TPU v7x, 32 devices: a whole 2x2x4 slice. The times are simulated.
32 devices in a mesh: front: 2 (over x), column: 4 (over y, core), row: 4 (over z).
Axes of the slice: x: 2, y: 2, z: 4, core: 2. Of those that a mesh axis runs over, the one named last changes fastest.
Arguments:
- cbs: float32 [2, 2, 2048, 2048], P('front', None, 'row', 'column'), may hold values from -4 to 4
- row_map: int32 [2, 2, 16], P('front'), may hold values from 0 to 47, as said below
- col_map: int32 [2, 2, 16], P('front'), may hold values from 0 to 47, as said below
- child_size: int32 [2, 2], P('front'), may hold values from 8 to 16, as said below
- front_diag: float32 [2, 6144], P('front'), may hold values from 0.1 to 200
- panel_order: int32 [2, 4], P('front'), may hold values from 0 to 23, as said below
- pivot_inverse: float32 [2, 4, 256, 256], P('front'), may hold values from -0.2 to 0.8
Outputs:
- factored_front: float32 [2, 6144, 6144], P('front', 'row', 'column')
Inputs may be any that keep to these rules, and one draw needn't show every extreme that they name: `row_map`: entries of one child are distinct. Split the parent tiles into aligned runs of 12 consecutive tiles (tiles t with the same t // 12, the tiles one row owner holds). In each aligned run of 4 entries at most 2 lie in one such aligned parent run, and in every aligned run of 4 entries some aligned parent run gets exactly 2. `col_map`: entries of one child are distinct. Split the parent tiles into aligned runs of 12 consecutive tiles (tiles t with the same t // 12, the tiles one column owner holds). In each aligned run of 4 entries no two lie in the same such aligned parent run. `child_size`: every front has a child of size 16. `panel_order`: distinct within a front. The first and the last panel block are each eliminated by exactly one front.
All inputs are finite; a program needn't handle non-finite values.
Results may differ from a plain program's by a relative error of at most 0.0003.
Values sent between devices are 32-bit elements; how exact they have to be, the bound alone decides.
No kernel may reach another device: no remote copies, remote signals or barrier semaphores. Data moves between devices by JAX's collectives and lax.ppermute only.
A program may use at most 192 MiB of HBM per device.

v0:
```python
import jax
import jax.numpy as jnp
from jax import lax
from jax.sharding import PartitionSpec as P

ORDER = 6144
TILE = 128
PANEL = 256
PANELS = 4
ROWMOST = 2


HIGHEST = lax.Precision.HIGHEST


def broadcast(block, axis, source):
    block = jnp.where(lax.axis_index(axis) == source, block, jnp.zeros_like(block))
    return lax.psum(block, axis)


def pack_tiles(tile_stack, target_dev, target_spot, dest_count, capacity, sentinel):
    dest_iota = jnp.arange(dest_count, dtype=jnp.int32)
    matches = (target_dev[:, None] == dest_iota[None, :]).astype(jnp.int32)
    earlier = jnp.cumsum(matches, axis=0) - matches
    position = jnp.sum(earlier * matches, axis=1)
    usable = target_dev < dest_count
    slot_index = jnp.where(usable, target_dev * capacity + position, dest_count * capacity)
    payload = jnp.zeros((dest_count * capacity,) + tile_stack.shape[1:], tile_stack.dtype)
    payload = payload.at[slot_index].set(tile_stack, mode="drop")
    labels = (
        jnp.full((dest_count * capacity,), sentinel, jnp.int32)
        .at[slot_index]
        .set(target_spot, mode="drop")
    )
    return (
        payload.reshape((dest_count, capacity) + tile_stack.shape[1:]),
        labels.reshape(dest_count, capacity),
    )


def scatter_tiles(payload, labels, row_tiles, col_tiles):
    tile_side = payload.shape[-1]
    tile_grid = jnp.zeros((row_tiles * col_tiles + 1, tile_side, tile_side), jnp.float32)
    tile_grid = tile_grid.at[labels.reshape(-1)].add(payload.reshape(-1, tile_side, tile_side))
    tile_grid = tile_grid[: row_tiles * col_tiles]
    tile_grid = tile_grid.reshape(row_tiles, col_tiles, tile_side, tile_side).transpose(0, 2, 1, 3)
    return tile_grid.reshape(row_tiles * tile_side, col_tiles * tile_side)


def body(cbs, row_map, col_map, child_size, front_diag, panel_order, pivot_inverse):
    groups = lax.axis_size("front")
    row_devs = lax.axis_size("row")
    col_devs = lax.axis_size("column")
    row_id = lax.axis_index("row")
    col_id = lax.axis_index("column")
    children = cbs.shape[1]
    piece_rows = cbs.shape[2] // TILE
    piece_cols = cbs.shape[3] // TILE
    local_rows = ORDER // row_devs
    local_cols = ORDER // col_devs
    row_tiles = local_rows // TILE
    col_tiles = local_cols // TILE
    sentinel = row_tiles * col_tiles
    tile_stack = (
        cbs[0].reshape(children, piece_rows, TILE, piece_cols, TILE).transpose(0, 1, 3, 2, 4)
    )
    tile_stack = tile_stack.reshape(-1, TILE, TILE)
    child_rows = row_id * piece_rows + jnp.arange(piece_rows, dtype=jnp.int32)
    child_cols = col_id * piece_cols + jnp.arange(piece_cols, dtype=jnp.int32)
    parent_rows = lax.dynamic_slice_in_dim(row_map[0], row_id * piece_rows, piece_rows, 1)
    parent_cols = lax.dynamic_slice_in_dim(col_map[0], col_id * piece_cols, piece_cols, 1)
    live_rows = child_rows[None, :] < child_size[0][:, None]
    live_cols = child_cols[None, :] < child_size[0][:, None]
    owner_rows = parent_rows // row_tiles
    owner_cols = parent_cols // col_tiles
    target_spot = (
        (parent_rows - owner_rows * row_tiles)[:, :, None] * col_tiles
        + (parent_cols - owner_cols * col_tiles)[:, None, :]
    ).reshape(-1)
    usable = (live_rows[:, :, None] & live_cols[:, None, :]).reshape(-1)
    inner_dest = (owner_cols[:, None, :] * row_devs + owner_rows[:, :, None]).reshape(-1)
    all_devices = groups * row_devs * col_devs
    front_ids = jnp.arange(children, dtype=jnp.int32)[:, None]
    whole_dest = (front_ids * (row_devs * col_devs) + inner_dest.reshape(children, -1)).reshape(-1)
    whole_target = jnp.where(usable, whole_dest, all_devices)
    payload, labels = pack_tiles(
        tile_stack, whole_target, target_spot, all_devices, ROWMOST, sentinel
    )
    arrived, arrived_labels = (
        lax.all_to_all(
            payload, ("front", "column", "row"), split_axis=0, concat_axis=0, tiled=True
        ),
        lax.all_to_all(labels, ("front", "column", "row"), split_axis=0, concat_axis=0, tiled=True),
    )
    matrix = scatter_tiles(arrived, arrived_labels, row_tiles, col_tiles)
    row_glob = row_id * local_rows + jnp.arange(local_rows, dtype=jnp.int32)
    col_glob = col_id * local_cols + jnp.arange(local_cols, dtype=jnp.int32)
    diag_part = lax.dynamic_slice_in_dim(front_diag[0], row_id * local_rows, local_rows)
    matrix = matrix + jnp.where(row_glob[:, None] == col_glob[None, :], diag_part[:, None], 0.0)
    order_row = panel_order[0]
    inverses = pivot_inverse[0]
    panel_rows = local_rows // PANEL
    panel_cols = local_cols // PANEL
    row_block = row_glob // PANEL
    col_block = col_glob // PANEL

    def strip_bounds(step_index):
        pivot_block = order_row[step_index]
        return (
            pivot_block // panel_cols,
            pivot_block // panel_rows,
            pivot_block % panel_cols * PANEL,
            pivot_block % panel_rows * PANEL,
        )

    def actives(step_index):
        chosen = order_row[: step_index + 1]
        active_rows = jnp.all(row_block[:, None] != chosen[None, :], axis=1)
        active_cols = jnp.all(col_block[:, None] != chosen[None, :], axis=1)
        return (active_rows, active_cols)

    def current_strips(matrix, step_index):
        col_owner, row_owner, col_offset, row_offset = strip_bounds(step_index)
        return (
            lax.dynamic_slice_in_dim(matrix, col_offset, PANEL, 1),
            lax.dynamic_slice_in_dim(matrix, row_offset, PANEL, 0),
        )

    def share_strips(col_strip, row_strip, step_index):
        col_owner, row_owner, col_offset, row_offset = strip_bounds(step_index)
        owner_left = jnp.dot(
            col_strip, inverses[step_index], precision=HIGHEST, preferred_element_type=jnp.float32
        )
        left_strip = broadcast(owner_left, "column", col_owner)
        top_strip = broadcast(row_strip, "row", row_owner)
        return (left_strip, top_strip)

    first_col, first_row = current_strips(matrix, 0)
    left_strip, top_strip = share_strips(first_col, first_row, 0)
    for step_index in range(PANELS):
        if step_index + 1 < PANELS:
            active_rows, active_cols = actives(step_index)
            next_col, next_row = current_strips(matrix, step_index + 1)
            col_owner, row_owner, col_offset, row_offset = strip_bounds(step_index + 1)
            top_part = lax.dynamic_slice_in_dim(top_strip, col_offset, PANEL, 1)
            left_part = lax.dynamic_slice_in_dim(left_strip, row_offset, PANEL, 0)
            next_col = jnp.where(
                active_rows[:, None],
                next_col
                - jnp.dot(
                    left_strip, top_part, precision=HIGHEST, preferred_element_type=jnp.float32
                ),
                next_col,
            )
            next_row = jnp.where(
                active_cols[None, :],
                next_row
                - jnp.dot(
                    left_part, top_strip, precision=HIGHEST, preferred_element_type=jnp.float32
                ),
                next_row,
            )
            left_next, top_next = share_strips(next_col, next_row, step_index + 1)
        eliminate_matrix = matrix
        eliminate_active_rows, eliminate_active_cols = actives(step_index)
        product = jnp.dot(
            left_strip, top_strip, precision=HIGHEST, preferred_element_type=jnp.float32
        )
        eliminate_matrix = jnp.where(
            eliminate_active_rows[:, None] & eliminate_active_cols[None, :],
            eliminate_matrix - product,
            eliminate_matrix,
        )
        eliminate_col_owner, eliminate_row_owner, eliminate_col_offset, eliminate_row_offset = (
            strip_bounds(step_index)
        )
        present = lax.dynamic_slice_in_dim(eliminate_matrix, eliminate_col_offset, PANEL, 1)
        fresh_col = jnp.where(
            (col_id == eliminate_col_owner) & eliminate_active_rows[:, None], left_strip, present
        )
        matrix = lax.dynamic_update_slice_in_dim(
            eliminate_matrix, fresh_col, eliminate_col_offset, 1
        )
        if step_index + 1 < PANELS:
            left_strip, top_strip = (left_next, top_next)
    return matrix[None]


def solution(mesh):
    placed = (
        P("front", None, "row", "column"),
        P("front", None, None),
        P("front", None, None),
        P("front", None),
        P("front", None),
        P("front", None),
        P("front", None, None, None),
    )
    return jax.shard_map(
        body, mesh=mesh, in_specs=placed, out_specs=P("front", "row", "column"), check_vma=False
    )
```

profile of v0, /device:TPU:0, one launch (start us, length us, event | category | flops | bytes accessed | tf_op | source)
XLA Modules:
  0.0 677.5 jit_solution(4158527166542845537)
XLA Ops:
  6.5 0.7 broadcast_compare_fusion.3
  7.8 0.8 multiply_subtract_fusion
  10.0 0.7 all_to_all.9
  10.7 7.3 %all-to-all-start = ((s32[32,1,2]{2,1,0:T(1,128)}), s32[32,1,2]{2,1,0:T(1,128)S(1)}, u32[]{:S(2)}, u32[]{:S(2)}) async-start(s32[32,1,2]{2,1,0:T(1,128)} %bitcast.9), calls=%async_computation | async-start | bytes 32768 | tf_op jit(solution)/shard_map/all_to_all | solution.py:93
  18.0 2.9 reshape_squeeze.3
  20.9 1.9 copy.15
  22.8 2.5 broadcast_in_dim.159
  25.3 5.3 scatter_fusion
  30.7 6.0 all-to-all-start.1
  39.9 0.7 reduce.5
  40.8 86.3 %all-to-all-done.1 = f32[32,2,128,128]{3,2,1,0:T(8,128)} async-done(((f32[32,2,128,128]{3,2,1,0:T(8,128)}), f32[32,2,128,128]{3,2,1,0:T(8,128)}, u32[]{:S(2)}, u32[]{:S(2)}) %all-to-all-start.1) | async-done | bytes 4194336 | tf_op jit(solution)/shard_map/all_to_all | solution.py:90
  127.1 4.8 broadcast_in_dim.154
  132.0 14.4 %scatter_fusion.1 = f32[145,128,128]{2,1,0:T(8,128)} fusion(f32[145,128,128]{2,1,0:T(8,128)} %broadcast_in_dim.154, s32[64]{0:T(128)S(1)} %fusion.41, f32[64,128,128]{2,1,0:T(8,128)} %bitcast.14), kind=kCustom, calls=%fused_computation.2 | custom fusion | flops 1048576 | bytes 12583168 | tf_op jit(solution)/shard_map/scatter-add | solution.py:44
  146.4 8.8 %slice.69 = f32[144,128,128]{2,1,0:T(8,128)} slice(f32[145,128,128]{2,1,0:T(8,128)} %scatter_fusion.1), slice={[0:144], [0:128], [0:128]} | slice | bytes 18874368 | tf_op jit(solution)/shard_map/slice | solution.py:45
  155.2 9.9 %copy.16 = f32[12,128,12,128]{3,2,1,0:T(8,128)S(1)} copy(f32[12,128,12,128]{3,1,2,0:T(8,128)} %bitcast.90) | data formatting | bytes 18874368 | tf_op jit(solution)/shard_map/transpose | solution.py:46
  165.1 3.1 bitcast_add_fusion
  168.3 3.7 copy-done.2
  172.0 3.7 convolution_select_fusion.3
  175.8 2.7 dynamic-slice_select_fusion
  180.8 38.8 %all-reduce.9.cloned.1.call-done = f32[1536,256]{1,0:T(8,128)} async-done(((f32[1536,256]{1,0:T(8,128)}), f32[1536,256]{1,0:T(8,128)}) %all-reduce.9.cloned.1.call-update) | async-done | bytes 1572880 | tf_op jit(solution)/shard_map/psum | solution.py:18
  219.7 71.6 %all-reduce.11.cloned.1.call-done = f32[256,1536]{1,0:T(8,128)} async-done(((f32[256,1536]{1,0:T(8,128)}), f32[256,1536]{1,0:T(8,128)}) %all-reduce.11.cloned.1.call-update) | async-done | bytes 1572880 | tf_op jit(solution)/shard_map/psum | solution.py:18
  291.2 3.4 fusion.8
  294.7 3.6 convolution_select_fusion.2
  298.4 0.8 broadcast_compare_fusion
  299.7 4.1 fusion.7
  306.7 12.5 %subtract_select_fusion.3 = f32[1536,1536]{1,0:T(8,128)} fusion(f32[1536,1536]{1,0:T(8,128)} %copy-done.2, f32[1536,256]{1,0:T(8,128)S(1)} %copy-done.4, f32[256,1536]{1,0:T(8,128)S(1)} %copy-done.7, pred[1536]{0:T(1024)(128)(4,1)S(1)} %broadcast_compare_fusion, pred[1536]{0:T(1024)(128)(4,1)S(1)} %broadcast_compare_fusion.1), kind=kOutput, calls=%fused_computation.6 | convolution fusion | flops 7254835200 | bytes 22023168 | tf_op jit(solution)/shard_map/dot_general | solution.py:166
  319.2 2.9 select_dynamic-update-slice_fusion.2
  322.1 18.2 %all-reduce.13.cloned.1.call-done = f32[1536,256]{1,0:T(8,128)} async-done(((f32[1536,256]{1,0:T(8,128)}), f32[1536,256]{1,0:T(8,128)}) %all-reduce.13.cloned.1.call-update) | async-done | bytes 1572880 | tf_op jit(solution)/shard_map/psum | solution.py:18
  340.3 71.4 %all-reduce.15.cloned.1.call-done = f32[256,1536]{1,0:T(8,128)} async-done(((f32[256,1536]{1,0:T(8,128)}), f32[256,1536]{1,0:T(8,128)}) %all-reduce.15.cloned.1.call-update) | async-done | bytes 1572880 | tf_op jit(solution)/shard_map/psum | solution.py:18
  411.8 3.4 fusion.5
  415.2 3.6 convolution_select_fusion.1
  419.3 0.9 copy-done.3
  420.2 4.1 fusion.4
  426.2 12.5 %subtract_select_fusion.2 = f32[1536,1536]{1,0:T(8,128)} fusion(f32[1536,1536]{1,0:T(8,128)} %select_dynamic-update-slice_fusion.2, f32[1536,256]{1,0:T(8,128)S(1)} %copy-done.3, f32[256,1536]{1,0:T(8,128)S(1)} %copy-done.6, pred[1536]{0:T(1024)(128)(4,1)S(1)} %get-tuple-element.10, pred[1536]{0:T(1024)(128)(4,1)S(1)} %get-tuple-element.9), kind=kOutput, calls=%fused_computation.5 | convolution fusion | flops 7254835200 | bytes 22023168 | tf_op jit(solution)/shard_map/dot_general | solution.py:166
  438.7 2.9 select_dynamic-update-slice_fusion.1
  441.7 19.3 %all-reduce.17.cloned.1.call-done = f32[1536,256]{1,0:T(8,128)} async-done(((f32[1536,256]{1,0:T(8,128)}), f32[1536,256]{1,0:T(8,128)}) %all-reduce.17.cloned.1.call-update) | async-done | bytes 1572880 | tf_op jit(solution)/shard_map/psum | solution.py:18
  460.9 71.4 %all-reduce.19.cloned.1.call-done = f32[256,1536]{1,0:T(8,128)} async-done(((f32[256,1536]{1,0:T(8,128)}), f32[256,1536]{1,0:T(8,128)}) %all-reduce.19.cloned.1.call-update) | async-done | bytes 1572880 | tf_op jit(solution)/shard_map/psum | solution.py:18
  532.3 3.4 fusion.2
  535.8 3.6 convolution_select_fusion
  539.7 1.1 copy-done.5
  540.8 4.1 fusion.1
  545.1 12.5 %subtract_select_fusion.1 = f32[1536,1536]{1,0:T(8,128)} fusion(f32[1536,1536]{1,0:T(8,128)} %select_dynamic-update-slice_fusion.1, f32[1536,256]{1,0:T(8,128)S(1)} %copy-done.5, f32[256,1536]{1,0:T(8,128)S(1)} %copy-done.8, pred[1536]{0:T(1024)(128)(4,1)S(1)} %get-tuple-element.8, pred[1536]{0:T(1024)(128)(4,1)S(1)} %get-tuple-element.7), kind=kOutput, calls=%fused_computation.4 | convolution fusion | flops 7254835200 | bytes 22023168 | tf_op jit(solution)/shard_map/dot_general | solution.py:166
  557.5 2.9 select_dynamic-update-slice_fusion
  560.5 21.0 %all-reduce.21.cloned.1.call-done = f32[1536,256]{1,0:T(8,128)} async-done(((f32[1536,256]{1,0:T(8,128)}), f32[1536,256]{1,0:T(8,128)}) %all-reduce.21.cloned.1.call-update) | async-done | bytes 1572880 | tf_op jit(solution)/shard_map/psum | solution.py:18
  581.5 71.6 %all-reduce.23.cloned.1.call-done = f32[256,1536]{1,0:T(8,128)} async-done(((f32[256,1536]{1,0:T(8,128)}), f32[256,1536]{1,0:T(8,128)}) %all-reduce.23.cloned.1.call-update) | async-done | bytes 1572880 | tf_op jit(solution)/shard_map/psum | solution.py:18
  653.1 12.2 %subtract_select_fusion = f32[1536,1536]{1,0:T(8,128)S(1)} fusion(f32[1536,1536]{1,0:T(8,128)} %select_dynamic-update-slice_fusion, f32[1536,256]{1,0:T(8,128)} %all-reduce.21.cloned.1.call-done, f32[256,1536]{1,0:T(8,128)} %all-reduce.23.cloned.1.call-done, pred[1536]{0:T(1024)(128)(4,1)S(1)} %get-tuple-element.6, pred[1536]{0:T(1024)(128)(4,1)S(1)} %get-tuple-element.5), kind=kOutput, calls=%fused_computation.3 | convolution fusion | flops 7254835200 | bytes 22023168 | tf_op jit(solution)/shard_map/dot_general | solution.py:166
  665.3 3.7 copy.32
  669.1 1.4 bitcast_dynamic-update-slice_fusion
  (74 shorter events, 6.6 us)
Async XLA Ops:
  6.5 32.8 %copy-start = (f32[1,6144]{1,0:T(1,128)S(1)}, f32[1,6144]{1,0:T(1,128)}, u32[]{:S(2)}) copy-start(f32[1,6144]{1,0:T(1,128)} %param.11) | copy-start | bytes 73732
  10.7 19.9 %all-to-all-start = ((s32[32,1,2]{2,1,0:T(1,128)}), s32[32,1,2]{2,1,0:T(1,128)S(1)}, u32[]{:S(2)}, u32[]{:S(2)}) async-start(s32[32,1,2]{2,1,0:T(1,128)} %bitcast.9), calls=%async_computation | async-start | bytes 32768 | tf_op jit(solution)/shard_map/all_to_all | solution.py:93
  30.7 6.0 copy-start.10
  30.7 96.5 %all-to-all-start.1 = ((f32[32,2,128,128]{3,2,1,0:T(8,128)}), f32[32,2,128,128]{3,2,1,0:T(8,128)}, u32[]{:S(2)}, u32[]{:S(2)}) async-start(f32[32,2,128,128]{3,2,1,0:T(8,128)} %bitcast.91), calls=%async_computation.1 | async-start | bytes 8388608 | tf_op jit(solution)/shard_map/all_to_all | solution.py:90
  36.6 183.0 %all-reduce.9.cloned.1.call-start = ((), (), s32[]{:S(2)}) async-start(), calls=%async_computation.2 | async-start | bytes 3145728 | tf_op jit(solution)/shard_map/psum | solution.py:18
  168.2 3.7 copy-start.2
  175.7 115.5 %all-reduce.11.cloned.1.call-start = ((), (), s32[]{:S(2)}) async-start(), calls=%async_computation.3 | async-start | bytes 3145728 | tf_op jit(solution)/shard_map/psum | solution.py:18
  178.5 161.9 %all-reduce.13.cloned.1.call-start = ((), (), s32[]{:S(2)}) async-start(), calls=%async_computation.4 | async-start | bytes 3145728 | tf_op jit(solution)/shard_map/psum | solution.py:18
  294.7 4.5 copy-start.7
  298.3 1.4 copy-start.4
  298.3 113.5 %all-reduce.15.cloned.1.call-start = ((), (), s32[]{:S(2)}) async-start(), calls=%async_computation.5 | async-start | bytes 3145728 | tf_op jit(solution)/shard_map/psum | solution.py:18
  303.8 157.1 %all-reduce.17.cloned.1.call-start = ((), (), s32[]{:S(2)}) async-start(), calls=%async_computation.6 | async-start | bytes 3145728 | tf_op jit(solution)/shard_map/psum | solution.py:18
  415.2 4.1 copy-start.6
  418.8 1.4 copy-start.3
  418.8 113.5 %all-reduce.19.cloned.1.call-start = ((), (), s32[]{:S(2)}) async-start(), calls=%async_computation.7 | async-start | bytes 3145728 | tf_op jit(solution)/shard_map/psum | solution.py:18
  424.4 157.1 %all-reduce.21.cloned.1.call-start = ((), (), s32[]{:S(2)}) async-start(), calls=%async_computation.8 | async-start | bytes 3145728 | tf_op jit(solution)/shard_map/psum | solution.py:18
  535.8 3.9 copy-start.8
  539.4 1.4 copy-start.5
  539.4 113.6 %all-reduce.23.cloned.1.call-start = ((), (), s32[]{:S(2)}) async-start(), calls=%async_computation.9 | async-start | bytes 3145728 | tf_op jit(solution)/shard_map/psum | solution.py:18
  665.3 3.8 copy-start.9
  665.3 5.2 copy-start.1
Sparse Core Ops, SparseCore 0:
  175.8 43.7 all-reduce.8
  222.0 69.1 all-reduce.10
  298.4 41.8 all-reduce.12
  342.6 69.1 all-reduce.14
  419.0 41.8 all-reduce.16
  463.1 69.1 all-reduce.18
  539.6 41.8 all-reduce.20
  583.9 69.1 all-reduce.22
where the time goes:
time: 683 us; the launch traced here: 678 us
  waiting for transfers between devices  470 us (69%)
  matrix products  86.8 us (13%)
  local copies, waits for them, and re-layouts  49.7 us (7%)
  other arithmetic  35.7 us (5%)
  between operations  21.4 us (3%)
  starting transfers between devices  14.2 us (2%)
    psum x8, waiting for transfers between devices, broadcast(): return lax.psum(block, axis)  383 us
    all_to_all x1, waiting for transfers between devices, body(): lax.all_to_all(payload, ('front', 'column', 'row'), split_axis=0, concat_...  86.3 us
    dot_general x4, matrix products, body(): jnp.dot(left_strip, top_strip, precision=HIGHEST, preferred_element_type=...  49.7 us
    dot_general x4, matrix products, share_strips(): jnp.dot(col_strip, inverses[step_index], precision=HIGHEST, preferred_ele...  14.6 us
    scatter-add x1, other arithmetic, scatter_tiles(): tile_grid.at[labels.reshape(-1)]  14.4 us
  transfers between devices with their start and end apart: 10, of which 9 were waited for; matrix products, arithmetic and copies ran while one was open for 12% of the time, Pallas kernels for 0%

commit v1 on v0

--- a/solution.py
+++ b/solution.py
@@ -16,6 +16,21 @@
 def broadcast(block, axis, source):
     block = jnp.where(lax.axis_index(axis) == source, block, jnp.zeros_like(block))
     return lax.psum(block, axis)
+
+
+def exchange_broadcast(block, axis, source):
+    size = lax.axis_size(axis)
+    if size & (size - 1):
+        return broadcast(block, axis, source)
+    index = lax.axis_index(axis)
+    distance = 1
+    while distance < size:
+        partner = [(i, i ^ distance) for i in range(size)]
+        received = lax.ppermute(block, axis, partner)
+        take = (source // distance) % 2 != (index // distance) % 2
+        block = jnp.where(take, received, block)
+        distance *= 2
+    return block
 
 
 def pack_tiles(tile_stack, target_dev, target_spot, dest_count, capacity, sentinel):
@@ -131,7 +146,7 @@
         owner_left = jnp.dot(
             col_strip, inverses[step_index], precision=HIGHEST, preferred_element_type=jnp.float32
         )
-        left_strip = broadcast(owner_left, "column", col_owner)
+        left_strip = exchange_broadcast(owner_left, "column", col_owner)
         top_strip = broadcast(row_strip, "row", row_owner)
         return (left_strip, top_strip)
 

time: 683 us -> 537 us (0.79)
  waiting for transfers between devices: 470 us -> 309 us
  other arithmetic: 35.7 us -> 47.1 us
  starting transfers between devices: 14.2 us -> 21.5 us
    psum x8 -> x4, waiting for transfers between devices: 383 us -> 156 us  [broadcast(): return lax.psum(block, axis)]
    ppermute x0 -> x8, waiting for transfers between devices: none -> 64.9 us  [exchange_broadcast(): received = lax.ppermute(block, axis, partner)]
    select_n x0 -> x7, other arithmetic: none -> 12.4 us  [exchange_broadcast(): block = jnp.where(take, received, block)]
    ppermute x0 -> x8, starting transfers between devices: none -> 7.84 us  [exchange_broadcast(): received = lax.ppermute(block, axis, partner)]
  transfers between devices with their start and end apart: 10 -> 14, of which waited for: 9 -> 11; matrix products, arithmetic and copies ran while one was open for 12% -> 16% of each run, Pallas kernels for 0% -> 0%
where the time goes in v1:
time: 537 us; the launch traced here: 531 us
  waiting for transfers between devices  309 us (58%)
  matrix products  85.1 us (16%)
  local copies, waits for them, and re-layouts  47.1 us (9%)
  other arithmetic  47.1 us (9%)
  starting transfers between devices  21.5 us (4%)
  between operations  21.4 us (4%)
    psum x4, waiting for transfers between devices, broadcast(): return lax.psum(block, axis)  156 us
    all_to_all x1, waiting for transfers between devices, body(): lax.all_to_all(payload, ('front', 'column', 'row'), split_axis=0, concat_...  87.6 us
    ppermute x8, waiting for transfers between devices, exchange_broadcast(): received = lax.ppermute(block, axis, partner)  64.9 us
    dot_general x4, matrix products, body(): jnp.dot(left_strip, top_strip, precision=HIGHEST, preferred_element_type=...  50.5 us
    scatter-add x1, other arithmetic, scatter_tiles(): tile_grid.at[labels.reshape(-1)]  13.5 us
    dot_general x4, matrix products, share_strips(): jnp.dot(col_strip, inverses[step_index], precision=HIGHEST, preferred_ele...  13.4 us
    select_n x7, other arithmetic, exchange_broadcast(): block = jnp.where(take, received, block)  12.4 us
    dot_general x3, matrix products, body(): jnp.dot(left_part, top_strip, precision=HIGHEST, preferred_element_type=j...  12.3 us
  transfers between devices with their start and end apart: 14, of which 11 were waited for; matrix products, arithmetic and copies ran while one was open for 16% of the time, Pallas kernels for 0%

profile of v1, /device:TPU:0, one launch (start us, length us, event | category | flops | bytes accessed | tf_op | source)
XLA Modules:
  0.0 531.0 jit_solution(1873090798040778720)
XLA Ops:
  10.7 7.3 %all-to-all-start = ((s32[32,1,2]{2,1,0:T(1,128)}), s32[32,1,2]{2,1,0:T(1,128)S(1)}, u32[]{:S(2)}, u32[]{:S(2)}) async-start(s32[32,1,2]{2,1,0:T(1,128)} %bitcast.9), calls=%async_computation | async-start | bytes 32768 | tf_op jit(solution)/shard_map/all_to_all | solution.py:108
  18.0 2.9 reshape_squeeze.3
  20.9 1.9 copy.15
  22.8 2.5 broadcast_in_dim.159
  25.3 5.3 %scatter_fusion = f32[64,128,128]{2,1,0:T(8,128)} fusion(f32[64,128,128]{2,1,0:T(8,128)} %broadcast_in_dim.159, s32[32]{0:T(128)S(1)} %fusion.46, f32[32,128,128]{2,1,0:T(8,128)S(1)} %bitcast.91), kind=kCustom, calls=%fused_computation.1 | custom fusion | bytes 6291584 | tf_op jit(solution)/shard_map/scatter | solution.py:44
  30.7 6.2 %all-to-all-start.1 = ((f32[32,2,128,128]{3,2,1,0:T(8,128)}), f32[32,2,128,128]{3,2,1,0:T(8,128)}, u32[]{:S(2)}, u32[]{:S(2)}) async-start(f32[32,2,128,128]{3,2,1,0:T(8,128)} %bitcast.90), calls=%async_computation.1 | async-start | bytes 8388608 | tf_op jit(solution)/shard_map/all_to_all | solution.py:105
  39.7 87.6 %all-to-all-done.1 = f32[32,2,128,128]{3,2,1,0:T(8,128)} async-done(((f32[32,2,128,128]{3,2,1,0:T(8,128)}), f32[32,2,128,128]{3,2,1,0:T(8,128)}, u32[]{:S(2)}, u32[]{:S(2)}) %all-to-all-start.1) | async-done | bytes 4194336 | tf_op jit(solution)/shard_map/all_to_all | solution.py:105
  127.3 4.8 broadcast_in_dim.154
  132.2 13.5 %scatter_fusion.1 = f32[145,128,128]{2,1,0:T(8,128)} fusion(f32[145,128,128]{2,1,0:T(8,128)} %broadcast_in_dim.154, s32[64]{0:T(128)S(1)} %fusion.45, f32[64,128,128]{2,1,0:T(8,128)} %bitcast.14), kind=kCustom, calls=%fused_computation.2 | custom fusion | flops 1048576 | bytes 12583168 | tf_op jit(solution)/shard_map/scatter-add | solution.py:59
  145.6 8.8 %slice.69 = f32[144,128,128]{2,1,0:T(8,128)} slice(f32[145,128,128]{2,1,0:T(8,128)} %scatter_fusion.1), slice={[0:144], [0:128], [0:128]} | slice | bytes 18874368 | tf_op jit(solution)/shard_map/slice | solution.py:60
  154.4 9.9 %copy.16 = f32[12,128,12,128]{3,2,1,0:T(8,128)S(1)} copy(f32[12,128,12,128]{3,1,2,0:T(8,128)} %bitcast.89) | data formatting | bytes 18874368 | tf_op jit(solution)/shard_map/transpose | solution.py:61
  164.4 3.1 bitcast_add_fusion
  167.5 3.7 copy-done.2
  171.2 2.8 fusion.9
  174.0 1.6 collective-permute-start
  177.0 1.9 collective-permute-done
  178.9 1.7 broadcast_select_fusion.6
  180.6 1.7 collective-permute-start.1
  182.3 2.6 dynamic-slice_select_fusion
  186.3 29.7 %collective-permute-done.1 = f32[1536,256]{1,0:T(8,128)} collective-permute-done((f32[1536,256]{1,0:T(8,128)S(1)}, f32[1536,256]{1,0:T(8,128)}, u32[]{:S(2)}, u32[]{:S(2)}) %collective-permute-start.1) | collective-permute-done | bytes 1572896 | tf_op jit(solution)/shard_map/ppermute | solution.py:29
  216.3 38.2 %all-reduce.5.cloned.1.call-done = f32[256,1536]{1,0:T(8,128)} async-done(((f32[256,1536]{1,0:T(8,128)}), f32[256,1536]{1,0:T(8,128)}) %all-reduce.5.cloned.1.call-update) | async-done | bytes 1572880 | tf_op jit(solution)/shard_map/psum | solution.py:18
  254.5 2.9 fusion.8
  257.5 3.5 fusion.15
  264.7 2.8 broadcast_select_fusion.4
  269.0 4.1 fusion.7
  273.2 12.4 %subtract_select_fusion.3 = f32[1536,1536]{1,0:T(8,128)} fusion(f32[1536,1536]{1,0:T(8,128)} %copy-done.2, f32[1536,256]{1,0:T(8,128)S(1)} %broadcast_select_fusion.7, f32[256,1536]{1,0:T(8,128)S(1)} %copy-done.3, pred[1536]{0:T(1024)(128)(4,1)S(1)} %broadcast_compare_fusion, pred[1536]{0:T(1024)(128)(4,1)S(1)} %broadcast_compare_fusion.1), kind=kOutput, calls=%fused_computation.6 | convolution fusion | flops 7254835200 | bytes 22023168 | tf_op jit(solution)/shard_map/dot_general | solution.py:181
  285.6 2.9 select_dynamic-update-slice_fusion.2
  288.6 15.8 %collective-permute-done.3 = f32[1536,256]{1,0:T(8,128)} collective-permute-done((f32[1536,256]{1,0:T(8,128)}, f32[1536,256]{1,0:T(8,128)}, u32[]{:S(2)}, u32[]{:S(2)}) %collective-permute-start.3) | collective-permute-done | bytes 1572896 | tf_op jit(solution)/shard_map/ppermute | solution.py:29
  304.4 1.6 broadcast_select_fusion.5
  306.0 34.6 %all-reduce.7.cloned.1.call-done = f32[256,1536]{1,0:T(8,128)} async-done(((f32[256,1536]{1,0:T(8,128)}), f32[256,1536]{1,0:T(8,128)}) %all-reduce.7.cloned.1.call-update) | async-done | bytes 1572880 | tf_op jit(solution)/shard_map/psum | solution.py:18
  340.6 2.9 fusion.5
  343.5 3.5 fusion.13
  349.2 1.6 collective-permute-done.4
  350.8 2.7 broadcast_select_fusion.2
  355.0 4.1 fusion.4
  359.2 12.6 %subtract_select_fusion.2 = f32[1536,1536]{1,0:T(8,128)} fusion(f32[1536,1536]{1,0:T(8,128)} %select_dynamic-update-slice_fusion.2, f32[1536,256]{1,0:T(8,128)S(1)} %broadcast_select_fusion.5, f32[256,1536]{1,0:T(8,128)S(1)} %copy-done.4, pred[1536]{0:T(1024)(128)(4,1)S(1)} %get-tuple-element.10, pred[1536]{0:T(1024)(128)(4,1)S(1)} %get-tuple-element.9), kind=kOutput, calls=%fused_computation.5 | convolution fusion | flops 7254835200 | bytes 22023168 | tf_op jit(solution)/shard_map/dot_general | solution.py:181
  371.8 2.9 select_dynamic-update-slice_fusion.1
  374.7 15.6 %collective-permute-done.5 = f32[1536,256]{1,0:T(8,128)} collective-permute-done((f32[1536,256]{1,0:T(8,128)}, f32[1536,256]{1,0:T(8,128)}, u32[]{:S(2)}, u32[]{:S(2)}) %collective-permute-start.5) | collective-permute-done | bytes 1572896 | tf_op jit(solution)/shard_map/ppermute | solution.py:29
  391.9 34.7 %all-reduce.9.cloned.1.call-done = f32[256,1536]{1,0:T(8,128)} async-done(((f32[256,1536]{1,0:T(8,128)}), f32[256,1536]{1,0:T(8,128)}) %all-reduce.9.cloned.1.call-update) | async-done | bytes 1572880 | tf_op jit(solution)/shard_map/psum | solution.py:18
  426.6 2.9 fusion.2
  429.5 3.6 fusion.11
  434.3 4.1 fusion.1
  438.5 1.6 broadcast_select_fusion
  441.8 13.5 %subtract_select_fusion.1 = f32[1536,1536]{1,0:T(8,128)} fusion(f32[1536,1536]{1,0:T(8,128)} %select_dynamic-update-slice_fusion.1, f32[1536,256]{1,0:T(8,128)S(1)} %broadcast_select_fusion.3, f32[256,1536]{1,0:T(8,128)} %all-reduce.9.cloned.1.call-done, pred[1536]{0:T(1024)(128)(4,1)S(1)} %get-tuple-element.8, pred[1536]{0:T(1024)(128)(4,1)S(1)} %get-tuple-element.7), kind=kOutput, calls=%fused_computation.4 | convolution fusion | flops 7254835200 | bytes 22023168 | tf_op jit(solution)/shard_map/dot_general | solution.py:181
  455.3 3.0 select_dynamic-update-slice_fusion
  458.2 48.7 %all-reduce.11.cloned.1.call-done = f32[256,1536]{1,0:T(8,128)} async-done(((f32[256,1536]{1,0:T(8,128)}), f32[256,1536]{1,0:T(8,128)}) %all-reduce.11.cloned.1.call-update) | async-done | bytes 1572880 | tf_op jit(solution)/shard_map/psum | solution.py:18
  506.9 12.0 %subtract_select_fusion = f32[1536,1536]{1,0:T(8,128)S(1)} fusion(f32[1536,1536]{1,0:T(8,128)} %select_dynamic-update-slice_fusion, f32[256,1536]{1,0:T(8,128)} %all-reduce.11.cloned.1.call-done, pred[1536]{0:T(1024)(128)(4,1)S(1)} %get-tuple-element.6, pred[1536]{0:T(1024)(128)(4,1)S(1)} %get-tuple-element.5, f32[1536,256]{1,0:T(8,128)} %collective-permute-done.7, ...), kind=kOutput, calls=%fused_computation.3 | convolution fusion | flops 7255228416 | bytes 23596032 | tf_op jit(solution)/shard_map/dot_general | solution.py:181
  519.0 3.7 copy.28
  (77 shorter events, 17.2 us)
Async XLA Ops:
  6.5 31.7 %copy-start = (f32[1,6144]{1,0:T(1,128)S(1)}, f32[1,6144]{1,0:T(1,128)}, u32[]{:S(2)}) copy-start(f32[1,6144]{1,0:T(1,128)} %param.11) | copy-start | bytes 73732
  10.7 19.9 %all-to-all-start = ((s32[32,1,2]{2,1,0:T(1,128)}), s32[32,1,2]{2,1,0:T(1,128)S(1)}, u32[]{:S(2)}, u32[]{:S(2)}) async-start(s32[32,1,2]{2,1,0:T(1,128)} %bitcast.9), calls=%async_computation | async-start | bytes 32768 | tf_op jit(solution)/shard_map/all_to_all | solution.py:108
  30.7 6.2 %copy-start.6 = (s32[1,4]{1,0:T(1,128)S(1)}, s32[1,4]{1,0:T(1,128)}, u32[]{:S(2)}) copy-start(s32[1,4]{1,0:T(1,128)} %param.12) | copy-start | bytes 52
  30.7 96.7 %all-to-all-start.1 = ((f32[32,2,128,128]{3,2,1,0:T(8,128)}), f32[32,2,128,128]{3,2,1,0:T(8,128)}, u32[]{:S(2)}, u32[]{:S(2)}) async-start(f32[32,2,128,128]{3,2,1,0:T(8,128)} %bitcast.90), calls=%async_computation.1 | async-start | bytes 8388608 | tf_op jit(solution)/shard_map/all_to_all | solution.py:105
  36.8 217.7 %all-reduce.5.cloned.1.call-start = ((), (), s32[]{:S(2)}) async-start(), calls=%async_computation.2 | async-start | bytes 3145728 | tf_op jit(solution)/shard_map/psum | solution.py:18
  167.5 3.7 copy-start.2
  174.0 4.8 collective-permute-start
  180.6 35.4 %collective-permute-start.1 = (f32[1536,256]{1,0:T(8,128)S(1)}, f32[1536,256]{1,0:T(8,128)}, u32[]{:S(2)}, u32[]{:S(2)}) collective-permute-start(f32[1536,256]{1,0:T(8,128)S(1)} %broadcast_select_fusion.6), channel_id=1, source_target_pairs={{0,8},{4,12},{8,0},{12,4},{1,9},{5,13},{9,1},{13,5},{2,10},{6,14},... | collective-permute-start | bytes 4718600 | tf_op jit(solution)/shard_map/ppermute | solution.py:29
  185.0 155.6 %all-reduce.7.cloned.1.call-start = ((), (), s32[]{:S(2)}) async-start(), calls=%async_computation.3 | async-start | bytes 3145728 | tf_op jit(solution)/shard_map/psum | solution.py:18
  261.0 3.8 collective-permute-start.2
  264.3 4.7 copy-start.3
  267.5 36.8 %collective-permute-start.3 = (f32[1536,256]{1,0:T(8,128)}, f32[1536,256]{1,0:T(8,128)}, u32[]{:S(2)}, u32[]{:S(2)}) collective-permute-start(f32[1536,256]{1,0:T(8,128)} %broadcast_select_fusion.4), channel_id=1, source_target_pairs={{0,8},{4,12},{8,0},{12,4},{1,9},{5,13},{9,1},{13,5},{2,10},{6,14},... | collective-permute-start | bytes 4718600 | tf_op jit(solution)/shard_map/ppermute | solution.py:29
  273.2 153.4 %all-reduce.9.cloned.1.call-start = ((), (), s32[]{:S(2)}) async-start(), calls=%async_computation.4 | async-start | bytes 3145728 | tf_op jit(solution)/shard_map/psum | solution.py:18
  347.0 3.8 collective-permute-start.4
  349.2 5.8 %copy-start.4 = (f32[256,1536]{1,0:T(8,128)S(1)}, f32[256,1536]{1,0:T(8,128)}, u32[]{:S(2)}) copy-start(f32[256,1536]{1,0:T(8,128)} %all-reduce.7.cloned.1.call-done) | copy-start | bytes 4718596
  353.5 36.8 %collective-permute-start.5 = (f32[1536,256]{1,0:T(8,128)}, f32[1536,256]{1,0:T(8,128)}, u32[]{:S(2)}, u32[]{:S(2)}) collective-permute-start(f32[1536,256]{1,0:T(8,128)} %broadcast_select_fusion.2), channel_id=1, source_target_pairs={{0,8},{4,12},{8,0},{12,4},{1,9},{5,13},{9,1},{13,5},{2,10},{6,14},... | collective-permute-start | bytes 4718600 | tf_op jit(solution)/shard_map/ppermute | solution.py:29
  359.2 147.8 %all-reduce.11.cloned.1.call-start = ((), (), s32[]{:S(2)}) async-start(), calls=%async_computation.5 | async-start | bytes 3145728 | tf_op jit(solution)/shard_map/psum | solution.py:18
  429.5 4.8 copy-start.5
  433.2 5.3 collective-permute-start.6
  440.1 66.8 %collective-permute-start.7 = (f32[1536,256]{1,0:T(8,128)S(1)}, f32[1536,256]{1,0:T(8,128)}, u32[]{:S(2)}, u32[]{:S(2)}) collective-permute-start(f32[1536,256]{1,0:T(8,128)S(1)} %broadcast_select_fusion), channel_id=1, source_target_pairs={{0,8},{4,12},{8,0},{12,4},{1,9},{5,13},{9,1},{13,5},{2,10},{6,14},... | collective-permute-start | bytes 4718600 | tf_op jit(solution)/shard_map/ppermute | solution.py:29
  522.7 1.5 copy-start.1
Sparse Core Ops, SparseCore 0:
  185.1 69.4 all-reduce.4
  273.3 67.2 all-reduce.6
  359.3 67.2 all-reduce.8
  438.6 68.3 all-reduce.10

commit v2 on v1

--- a/solution.py
+++ b/solution.py
@@ -147,7 +147,7 @@
             col_strip, inverses[step_index], precision=HIGHEST, preferred_element_type=jnp.float32
         )
         left_strip = exchange_broadcast(owner_left, "column", col_owner)
-        top_strip = broadcast(row_strip, "row", row_owner)
+        top_strip = exchange_broadcast(row_strip, "row", row_owner)
         return (left_strip, top_strip)
 
     first_col, first_row = current_strips(matrix, 0)

time: 537 us -> 654 us (1.22)
  waiting for transfers between devices: 309 us -> 446 us
  starting transfers between devices: 21.5 us -> 35.4 us
  matrix products: 85.1 us -> 72 us
  between operations: 21.4 us -> 8.57 us
    ppermute x8 -> x16, waiting for transfers between devices: 64.9 us -> 358 us  [exchange_broadcast(): received = lax.ppermute(block, axis, partner)]
    psum x4 -> x0, waiting for transfers between devices: 156 us -> none  [broadcast(): return lax.psum(block, axis)]
    ppermute x8 -> x16, starting transfers between devices: 7.84 us -> 22.3 us  [exchange_broadcast(): received = lax.ppermute(block, axis, partner)]
    dot_general x4, matrix products: 50.5 us -> 43.5 us  [body(): jnp.dot(left_strip, top_strip, precision=HIGHEST, preferred_element_type=...]
    select_n x7 -> x14, other arithmetic: 12.4 us -> 18 us  [exchange_broadcast(): block = jnp.where(take, received, block)]
  transfers between devices with their start and end apart: 14 -> 18, of which waited for: 11 -> 9; matrix products, arithmetic and copies ran while one was open for 16% -> 12% of each run, Pallas kernels for 0% -> 0%
where the time goes in v2:
time: 654 us; the launch traced here: 650 us
  waiting for transfers between devices  446 us (68%)
  matrix products  72 us (11%)
  other arithmetic  44.3 us (7%)
  local copies, waits for them, and re-layouts  43.5 us (7%)
  starting transfers between devices  35.4 us (5%)
  between operations  8.57 us (1%)
    ppermute x16, waiting for transfers between devices, exchange_broadcast(): received = lax.ppermute(block, axis, partner)  358 us
    all_to_all x1, waiting for transfers between devices, body(): lax.all_to_all(payload, ('front', 'column', 'row'), split_axis=0, concat_...  87.7 us
    dot_general x4, matrix products, body(): jnp.dot(left_strip, top_strip, precision=HIGHEST, preferred_element_type=...  43.5 us
    ppermute x16, starting transfers between devices, exchange_broadcast(): received = lax.ppermute(block, axis, partner)  22.3 us
    select_n x14, other arithmetic, exchange_broadcast(): block = jnp.where(take, received, block)  18 us
    scatter-add x1, other arithmetic, scatter_tiles(): tile_grid.at[labels.reshape(-1)]  13.7 us
    dot_general x4, matrix products, share_strips(): jnp.dot(col_strip, inverses[step_index], precision=HIGHEST, preferred_ele...  13.3 us
  transfers between devices with their start and end apart: 18, of which 9 were waited for; matrix products, arithmetic and copies ran while one was open for 12% of the time, Pallas kernels for 0%

profile of v2, /device:TPU:0, one launch (start us, length us, event | category | flops | bytes accessed | tf_op | source)
XLA Modules:
  0.0 649.6 jit_solution(2693951695074020107)
XLA Ops:
  4.2 7.3 %all-to-all-start = ((s32[32,1,2]{2,1,0:T(1,128)}), s32[32,1,2]{2,1,0:T(1,128)S(1)}, u32[]{:S(2)}, u32[]{:S(2)}) async-start(s32[32,1,2]{2,1,0:T(1,128)} %bitcast.9), calls=%async_computation | async-start | bytes 32768 | tf_op jit(solution)/shard_map/all_to_all | solution.py:108
  11.5 2.9 reshape_squeeze.3
  14.4 1.9 copy.15
  16.2 2.5 broadcast_in_dim.159
  18.8 5.3 scatter_fusion
  24.1 5.8 all-to-all-start.1
  32.8 87.7 %all-to-all-done.1 = f32[32,2,128,128]{3,2,1,0:T(8,128)} async-done(((f32[32,2,128,128]{3,2,1,0:T(8,128)}), f32[32,2,128,128]{3,2,1,0:T(8,128)}, u32[]{:S(2)}, u32[]{:S(2)}) %all-to-all-start.1) | async-done | bytes 4194336 | tf_op jit(solution)/shard_map/all_to_all | solution.py:105
  120.5 4.8 broadcast_in_dim.154
  125.3 13.7 %scatter_fusion.1 = f32[145,128,128]{2,1,0:T(8,128)} fusion(f32[145,128,128]{2,1,0:T(8,128)} %broadcast_in_dim.154, s32[64]{0:T(128)S(1)} %fusion.44, f32[64,128,128]{2,1,0:T(8,128)} %bitcast.14), kind=kCustom, calls=%fused_computation.2 | custom fusion | flops 1048576 | bytes 12583168 | tf_op jit(solution)/shard_map/scatter-add | solution.py:59
  139.0 8.8 %slice.69 = f32[144,128,128]{2,1,0:T(8,128)} slice(f32[145,128,128]{2,1,0:T(8,128)} %scatter_fusion.1), slice={[0:144], [0:128], [0:128]} | slice | bytes 18874368 | tf_op jit(solution)/shard_map/slice | solution.py:60
  147.8 9.9 %copy.16 = f32[12,128,12,128]{3,2,1,0:T(8,128)S(1)} copy(f32[12,128,12,128]{3,1,2,0:T(8,128)} %bitcast.88) | data formatting | bytes 18874368 | tf_op jit(solution)/shard_map/transpose | solution.py:61
  157.7 3.1 bitcast_add_fusion
  161.0 5.4 collective-permute-start.2
  166.4 2.8 fusion.7
  170.7 29.3 %collective-permute-done.2 = f32[256,1536]{1,0:T(8,128)} collective-permute-done((f32[256,1536]{1,0:T(8,128)S(1)}, f32[256,1536]{1,0:T(8,128)}, u32[]{:S(2)}, u32[]{:S(2)}) %collective-permute-start.2) | collective-permute-done | bytes 1572896 | tf_op jit(solution)/shard_map/ppermute | solution.py:29
  199.9 1.6 broadcast_select_fusion.11
  201.5 3.2 collective-permute-start.3
  208.5 63.9 %collective-permute-done.3 = f32[256,1536]{1,0:T(8,128)} collective-permute-done((f32[256,1536]{1,0:T(8,128)S(1)}, f32[256,1536]{1,0:T(8,128)}, u32[]{:S(2)}, u32[]{:S(2)}) %collective-permute-start.3) | collective-permute-done | bytes 1572896 | tf_op jit(solution)/shard_map/ppermute | solution.py:29
  272.7 1.6 broadcast_select_fusion.14
  274.4 2.9 fusion.5
  277.2 3.5 fusion.14
  281.4 4.1 fusion.4
  288.4 1.6 broadcast_select_fusion.9
  291.0 31.6 %collective-permute-done.6 = f32[256,1536]{1,0:T(8,128)} collective-permute-done((f32[256,1536]{1,0:T(8,128)}, f32[256,1536]{1,0:T(8,128)}, u32[]{:S(2)}, u32[]{:S(2)}) %collective-permute-start.6) | collective-permute-done | bytes 1572896 | tf_op jit(solution)/shard_map/ppermute | solution.py:29
  322.6 1.6 broadcast_select_fusion.7
  324.2 3.4 collective-permute-start.7
  327.6 11.7 %subtract_select_fusion.3 = f32[1536,1536]{1,0:T(8,128)S(1)} fusion(f32[1536,1536]{1,0:T(8,128)} %copy-done.2, f32[1536,256]{1,0:T(8,128)S(1)} %broadcast_select_fusion.14, f32[256,1536]{1,0:T(8,128)S(1)} %broadcast_select_fusion.12, pred[1536]{0:T(1024)(128)(4,1)S(1)} %broadcast_compare_fusion, pred[1536]{0:T(1024)(128)(4,1)S(1)} %broadcast_compare_fusion.1), kind=kOutput, calls=%fused_computation.6 | convolution fusion | flops 7254835200 | bytes 22023168 | tf_op jit(solution)/shard_map/dot_general | solution.py:181
  340.1 55.7 %collective-permute-done.7 = f32[256,1536]{1,0:T(8,128)S(1)} collective-permute-done((f32[256,1536]{1,0:T(8,128)S(1)}, f32[256,1536]{1,0:T(8,128)S(1)}, u32[]{:S(2)}, u32[]{:S(2)}) %collective-permute-start.7) | collective-permute-done | bytes 1572896 | tf_op jit(solution)/shard_map/ppermute | solution.py:29
  397.5 3.5 fusion.12
  401.0 2.6 fusion.2
  406.6 1.8 broadcast_select_fusion.5
  409.3 31.5 %collective-permute-done.10 = f32[256,1536]{1,0:T(8,128)} collective-permute-done((f32[256,1536]{1,0:T(8,128)}, f32[256,1536]{1,0:T(8,128)}, u32[]{:S(2)}, u32[]{:S(2)}) %collective-permute-start.10) | collective-permute-done | bytes 1572896 | tf_op jit(solution)/shard_map/ppermute | solution.py:29
  440.8 1.6 broadcast_select_fusion.3
  442.4 2.4 collective-permute-start.11
  444.8 8.7 %subtract_select_fusion.2 = f32[1536,1536]{1,0:T(8,128)S(1)} fusion(f32[1536,1536]{1,0:T(8,128)S(1)} %copy-done.4, f32[1536,256]{1,0:T(8,128)S(1)} %broadcast_select_fusion.10, f32[256,1536]{1,0:T(8,128)S(1)} %broadcast_select_fusion.8, pred[1536]{0:T(1024)(128)(4,1)S(1)} %get-tuple-element.10, pred[1536]{0:T(1024)(128)(4,1)S(1)} %get-tuple-element.9), kind=kOutput, calls=%fused_computation.5 | convolution fusion | flops 7254835200 | bytes 22023168 | tf_op jit(solution)/shard_map/dot_general | solution.py:181
  454.3 58.8 %collective-permute-done.11 = f32[256,1536]{1,0:T(8,128)S(1)} collective-permute-done((f32[256,1536]{1,0:T(8,128)S(1)}, f32[256,1536]{1,0:T(8,128)S(1)}, u32[]{:S(2)}, u32[]{:S(2)}) %collective-permute-start.11) | collective-permute-done | bytes 1572896 | tf_op jit(solution)/shard_map/ppermute | solution.py:29
  513.3 1.5 fusion.1
  514.8 3.5 fusion.10
  518.3 2.7 fusion
  522.8 2.8 broadcast_select_fusion.1
  526.4 31.6 %collective-permute-done.14 = f32[256,1536]{1,0:T(8,128)} collective-permute-done((f32[256,1536]{1,0:T(8,128)}, f32[256,1536]{1,0:T(8,128)}, u32[]{:S(2)}, u32[]{:S(2)}) %collective-permute-start.14) | collective-permute-done | bytes 1572896 | tf_op jit(solution)/shard_map/ppermute | solution.py:29
  558.1 2.8 broadcast_select_fusion
  560.8 2.3 collective-permute-start.15
  563.3 12.3 %subtract_select_fusion.1 = f32[1536,1536]{1,0:T(8,128)S(1)} fusion(f32[1536,1536]{1,0:T(8,128)} %copy-done.5, f32[1536,256]{1,0:T(8,128)S(1)} %broadcast_select_fusion.6, f32[256,1536]{1,0:T(8,128)S(1)} %broadcast_select_fusion.4, pred[1536]{0:T(1024)(128)(4,1)S(1)} %get-tuple-element.8, pred[1536]{0:T(1024)(128)(4,1)S(1)} %get-tuple-element.7), kind=kOutput, calls=%fused_computation.4 | convolution fusion | flops 7254835200 | bytes 22023168 | tf_op jit(solution)/shard_map/dot_general | solution.py:181
  576.1 55.7 %collective-permute-done.15 = f32[256,1536]{1,0:T(8,128)} collective-permute-done((f32[256,1536]{1,0:T(8,128)}, f32[256,1536]{1,0:T(8,128)}, u32[]{:S(2)}, u32[]{:S(2)}) %collective-permute-start.15) | collective-permute-done | bytes 1572896 | tf_op jit(solution)/shard_map/ppermute | solution.py:29
  631.8 10.8 %subtract_select_fusion = f32[1536,1536]{1,0:T(8,128)S(1)} fusion(f32[1536,1536]{1,0:T(8,128)S(1)} %select_dynamic-update-slice_fusion, pred[1536]{0:T(1024)(128)(4,1)S(1)} %get-tuple-element.6, pred[1536]{0:T(1024)(128)(4,1)S(1)} %get-tuple-element.5, f32[256,1536]{1,0:T(8,128)} %collective-permute-done.15, f32[256,1536]{1,0:T(8,128)} %broadcast_select_fusion, ...), kind=kOutput, calls=%fused_computation.3 | convolution fusion | flops 7255621632 | bytes 25168898 | tf_op jit(solution)/shard_map/dot_general | solution.py:181
  642.6 3.7 copy.24
  646.3 2.8 bitcast_dynamic-update-slice_fusion
  (88 shorter events, 19.8 us)
Async XLA Ops:
  0.0 31.3 %copy-start = (f32[1,6144]{1,0:T(1,128)S(1)}, f32[1,6144]{1,0:T(1,128)}, u32[]{:S(2)}) copy-start(f32[1,6144]{1,0:T(1,128)} %param.11) | copy-start | bytes 73732
  4.2 19.9 %all-to-all-start = ((s32[32,1,2]{2,1,0:T(1,128)}), s32[32,1,2]{2,1,0:T(1,128)S(1)}, u32[]{:S(2)}, u32[]{:S(2)}) async-start(s32[32,1,2]{2,1,0:T(1,128)} %bitcast.9), calls=%async_computation | async-start | bytes 32768 | tf_op jit(solution)/shard_map/all_to_all | solution.py:108
  24.1 5.8 copy-start.6
  24.1 96.3 %all-to-all-start.1 = ((f32[32,2,128,128]{3,2,1,0:T(8,128)}), f32[32,2,128,128]{3,2,1,0:T(8,128)}, u32[]{:S(2)}, u32[]{:S(2)}) async-start(f32[32,2,128,128]{3,2,1,0:T(8,128)} %bitcast.89), calls=%async_computation.1 | async-start | bytes 8388608 | tf_op jit(solution)/shard_map/all_to_all | solution.py:105
  160.9 5.6 copy-start.2
  161.0 38.9 %collective-permute-start.2 = (f32[256,1536]{1,0:T(8,128)S(1)}, f32[256,1536]{1,0:T(8,128)}, u32[]{:S(2)}, u32[]{:S(2)}) collective-permute-start(f32[256,1536]{1,0:T(8,128)S(1)} %constant_dynamic-slice_fusion), channel_id=1, source_target_pairs={{0,1},{1,0},{2,3},{3,2},{4,5},{5,4},{6,7},{7,6},{8,9},{9,8},{10,11... | collective-permute-start | bytes 4718600 | tf_op jit(solution)/shard_map/ppermute | solution.py:29
  169.2 35.5 %collective-permute-start = (f32[1536,256]{1,0:T(8,128)S(1)}, f32[1536,256]{1,0:T(8,128)}, u32[]{:S(2)}, u32[]{:S(2)}) collective-permute-start(f32[1536,256]{1,0:T(8,128)S(1)} %fusion.7), channel_id=1, source_target_pairs={{0,4},{4,0},{8,12},{12,8},{1,5},{5,1},{9,13},{13,9},{2,6},{6,2},{1... | collective-permute-start | bytes 4718600 | tf_op jit(solution)/shard_map/ppermute | solution.py:29
  201.5 70.9 %collective-permute-start.3 = (f32[256,1536]{1,0:T(8,128)S(1)}, f32[256,1536]{1,0:T(8,128)}, u32[]{:S(2)}, u32[]{:S(2)}) collective-permute-start(f32[256,1536]{1,0:T(8,128)S(1)} %broadcast_select_fusion.11), channel_id=1, source_target_pairs={{0,2},{1,3},{2,0},{3,1},{4,6},{5,7},{6,4},{7,5},{8,10},{9,11},{10,... | collective-permute-start | bytes 4718600 | tf_op jit(solution)/shard_map/ppermute | solution.py:29
  206.2 66.6 %collective-permute-start.1 = (f32[1536,256]{1,0:T(8,128)}, f32[1536,256]{1,0:T(8,128)}, u32[]{:S(2)}, u32[]{:S(2)}) collective-permute-start(f32[1536,256]{1,0:T(8,128)} %broadcast_select_fusion.13), channel_id=1, source_target_pairs={{0,8},{4,12},{8,0},{12,4},{1,9},{5,13},{9,1},{13,5},{2,10},{6,14},... | collective-permute-start | bytes 4718600 | tf_op jit(solution)/shard_map/ppermute | solution.py:29
  280.7 7.6 %collective-permute-start.4 = (f32[1536,256]{1,0:T(8,128)}, f32[1536,256]{1,0:T(8,128)}, u32[]{:S(2)}, u32[]{:S(2)}) collective-permute-start(f32[1536,256]{1,0:T(8,128)} %fusion.14), channel_id=1, source_target_pairs={{0,4},{4,0},{8,12},{12,8},{1,5},{5,1},{9,13},{13,9},{2,6},{6,2},{1... | collective-permute-start | bytes 4718600 | tf_op jit(solution)/shard_map/ppermute | solution.py:29
  285.5 37.1 %collective-permute-start.6 = (f32[256,1536]{1,0:T(8,128)}, f32[256,1536]{1,0:T(8,128)}, u32[]{:S(2)}, u32[]{:S(2)}) collective-permute-start(f32[256,1536]{1,0:T(8,128)} %fusion.4), channel_id=1, source_target_pairs={{0,1},{1,0},{2,3},{3,2},{4,5},{5,4},{6,7},{7,6},{8,9},{9,8},{10,11... | collective-permute-start | bytes 4718600 | tf_op jit(solution)/shard_map/ppermute | solution.py:29
  290.0 49.9 %collective-permute-start.5 = (f32[1536,256]{1,0:T(8,128)S(1)}, f32[1536,256]{1,0:T(8,128)S(1)}, u32[]{:S(2)}, u32[]{:S(2)}) collective-permute-start(f32[1536,256]{1,0:T(8,128)S(1)} %broadcast_select_fusion.9), channel_id=1, source_target_pairs={{0,8},{4,12},{8,0},{12,4},{1,9},{5,13},{9,1},{13,5},{2,10},{6,14},... | collective-permute-start | bytes 4718600 | tf_op jit(solution)/shard_map/ppermute | solution.py:29
  324.2 71.6 %collective-permute-start.7 = (f32[256,1536]{1,0:T(8,128)S(1)}, f32[256,1536]{1,0:T(8,128)S(1)}, u32[]{:S(2)}, u32[]{:S(2)}) collective-permute-start(f32[256,1536]{1,0:T(8,128)S(1)} %broadcast_select_fusion.7), channel_id=1, source_target_pairs={{0,2},{1,3},{2,0},{3,1},{4,6},{5,7},{6,4},{7,5},{8,10},{9,11},{10,... | collective-permute-start | bytes 4718600 | tf_op jit(solution)/shard_map/ppermute | solution.py:29
  339.9 61.1 %copy-start.3 = (f32[1536,1536]{1,0:T(8,128)}, f32[1536,1536]{1,0:T(8,128)S(1)}, u32[]{:S(2)}) copy-start(f32[1536,1536]{1,0:T(8,128)S(1)} %select_dynamic-update-slice_fusion.2) | copy-start | bytes 28311556
  401.0 5.5 collective-permute-start.8
  403.7 37.1 %collective-permute-start.10 = (f32[256,1536]{1,0:T(8,128)}, f32[256,1536]{1,0:T(8,128)}, u32[]{:S(2)}, u32[]{:S(2)}) collective-permute-start(f32[256,1536]{1,0:T(8,128)} %fusion.2), channel_id=1, source_target_pairs={{0,1},{1,0},{2,3},{3,2},{4,5},{5,4},{6,7},{7,6},{8,9},{9,8},{10,11... | collective-permute-start | bytes 4718600 | tf_op jit(solution)/shard_map/ppermute | solution.py:29
  406.6 38.3 %copy-start.4 = (f32[1536,1536]{1,0:T(8,128)S(1)}, f32[1536,1536]{1,0:T(8,128)}, u32[]{:S(2)}) copy-start(f32[1536,1536]{1,0:T(8,128)} %copy-done.3) | copy-start | bytes 28311556
  408.3 45.7 %collective-permute-start.9 = (f32[1536,256]{1,0:T(8,128)S(1)}, f32[1536,256]{1,0:T(8,128)S(1)}, u32[]{:S(2)}, u32[]{:S(2)}) collective-permute-start(f32[1536,256]{1,0:T(8,128)S(1)} %broadcast_select_fusion.5), channel_id=1, source_target_pairs={{0,8},{4,12},{8,0},{12,4},{1,9},{5,13},{9,1},{13,5},{2,10},{6,14},... | collective-permute-start | bytes 4718600 | tf_op jit(solution)/shard_map/ppermute | solution.py:29
  442.4 70.7 %collective-permute-start.11 = (f32[256,1536]{1,0:T(8,128)S(1)}, f32[256,1536]{1,0:T(8,128)S(1)}, u32[]{:S(2)}, u32[]{:S(2)}) collective-permute-start(f32[256,1536]{1,0:T(8,128)S(1)} %broadcast_select_fusion.3), channel_id=1, source_target_pairs={{0,2},{1,3},{2,0},{3,1},{4,6},{5,7},{6,4},{7,5},{8,10},{9,11},{10,... | collective-permute-start | bytes 4718600 | tf_op jit(solution)/shard_map/ppermute | solution.py:29
  454.1 64.3 %copy-start.5 = (f32[1536,1536]{1,0:T(8,128)}, f32[1536,1536]{1,0:T(8,128)S(1)}, u32[]{:S(2)}) copy-start(f32[1536,1536]{1,0:T(8,128)S(1)} %select_dynamic-update-slice_fusion.1) | copy-start | bytes 28311556
  518.3 4.5 collective-permute-start.12
  521.0 37.1 %collective-permute-start.14 = (f32[256,1536]{1,0:T(8,128)}, f32[256,1536]{1,0:T(8,128)}, u32[]{:S(2)}, u32[]{:S(2)}) collective-permute-start(f32[256,1536]{1,0:T(8,128)} %fusion), channel_id=1, source_target_pairs={{0,1},{1,0},{2,3},{3,2},{4,5},{5,4},{6,7},{7,6},{8,9},{9,8},{10,11... | collective-permute-start | bytes 4718600 | tf_op jit(solution)/shard_map/ppermute | solution.py:29
  525.6 50.5 %collective-permute-start.13 = (f32[1536,256]{1,0:T(8,128)}, f32[1536,256]{1,0:T(8,128)}, u32[]{:S(2)}, u32[]{:S(2)}) collective-permute-start(f32[1536,256]{1,0:T(8,128)} %broadcast_select_fusion.1), channel_id=1, source_target_pairs={{0,8},{4,12},{8,0},{12,4},{1,9},{5,13},{9,1},{13,5},{2,10},{6,14},... | collective-permute-start | bytes 4718600 | tf_op jit(solution)/shard_map/ppermute | solution.py:29
  560.8 70.9 %collective-permute-start.15 = (f32[256,1536]{1,0:T(8,128)}, f32[256,1536]{1,0:T(8,128)}, u32[]{:S(2)}, u32[]{:S(2)}) collective-permute-start(f32[256,1536]{1,0:T(8,128)} %broadcast_select_fusion), channel_id=1, source_target_pairs={{0,2},{1,3},{2,0},{3,1},{4,6},{5,7},{6,4},{7,5},{8,10},{9,11},{10,... | collective-permute-start | bytes 4718600 | tf_op jit(solution)/shard_map/ppermute | solution.py:29
  646.3 2.8 copy-start.1

commit v3 on v2

--- a/solution.py
+++ b/solution.py
@@ -147,7 +147,14 @@
             col_strip, inverses[step_index], precision=HIGHEST, preferred_element_type=jnp.float32
         )
         left_strip = exchange_broadcast(owner_left, "column", col_owner)
-        top_strip = exchange_broadcast(row_strip, "row", row_owner)
+        half_cols = row_strip.shape[1] // 2
+        top_strip = jnp.concatenate(
+            [
+                broadcast(row_strip[:, :half_cols], "row", row_owner),
+                exchange_broadcast(row_strip[:, half_cols:], "row", row_owner),
+            ],
+            axis=1,
+        )
         return (left_strip, top_strip)
 
     first_col, first_row = current_strips(matrix, 0)

time: 654 us -> 635 us (0.971)
  waiting for transfers between devices: 446 us -> 355 us
  other arithmetic: 44.3 us -> 69.6 us
  local copies, waits for them, and re-layouts: 43.5 us -> 64.7 us
  between operations: 8.57 us -> 22 us
  matrix products: 72 us -> 83.2 us
    ppermute x16, waiting for transfers between devices: 358 us -> 203 us  [exchange_broadcast(): received = lax.ppermute(block, axis, partner)]
    psum x0 -> x4, waiting for transfers between devices: none -> 63.3 us  [broadcast(): return lax.psum(block, axis)]
    reshape x0 -> x1, local copies, waits for them, and re-layouts: none -> 12.6 us  [scatter_tiles(): return tile_grid.reshape(row_tiles * tile_side, col_tiles * tile_side)]
    select_n x0 -> x4, other arithmetic: none -> 10.8 us  [broadcast(): jnp.where(lax.axis_index(axis) == source, block, jnp.zeros_like(block))]
    transpose x1 -> x0, local copies, waits for them, and re-layouts: 9.92 us -> none  [scatter_tiles(): tile_grid.reshape(row_tiles, col_tiles, tile_side, tile_side)]
    dynamic_update_slice x0 -> x1, local copies, waits for them, and re-layouts: none -> 9.59 us  [body(): lax.dynamic_update_slice_in_dim(eliminate_matrix, fresh_col, eliminate_co...]
    dot_general x4, matrix products: 43.5 us -> 51.2 us  [body(): jnp.dot(left_strip, top_strip, precision=HIGHEST, preferred_element_type=...]
    dynamic_update_slice x4, other arithmetic: 4.32 us -> 11.5 us  [body(): lax.dynamic_update_slice_in_dim(eliminate_matrix, fresh_col, eliminate_co...]
  transfers between devices with their start and end apart: 18 -> 22, of which waited for: 9 -> 13; matrix products, arithmetic and copies ran while one was open for 12% -> 17% of each run, Pallas kernels for 0% -> 0%
where the time goes in v3:
time: 635 us; the launch traced here: 627 us
  waiting for transfers between devices  355 us (56%)
  matrix products  83.2 us (13%)
  other arithmetic  69.6 us (11%)
  local copies, waits for them, and re-layouts  64.7 us (10%)
  starting transfers between devices  33 us (5%)
  between operations  22 us (3%)
    ppermute x16, waiting for transfers between devices, exchange_broadcast(): received = lax.ppermute(block, axis, partner)  203 us
    all_to_all x1, waiting for transfers between devices, body(): lax.all_to_all(payload, ('front', 'column', 'row'), split_axis=0, concat_...  87.7 us
    psum x4, waiting for transfers between devices, broadcast(): return lax.psum(block, axis)  63.3 us
    dot_general x4, matrix products, body(): jnp.dot(left_strip, top_strip, precision=HIGHEST, preferred_element_type=...  51.2 us
    select_n x12, other arithmetic, exchange_broadcast(): block = jnp.where(take, received, block)  20.2 us
    ppermute x16, starting transfers between devices, exchange_broadcast(): received = lax.ppermute(block, axis, partner)  19.1 us
    dot_general x4, matrix products, share_strips(): jnp.dot(col_strip, inverses[step_index], precision=HIGHEST, preferred_ele...  13.8 us
    scatter-add x1, other arithmetic, scatter_tiles(): tile_grid.at[labels.reshape(-1)]  13.6 us
  transfers between devices with their start and end apart: 22, of which 13 were waited for; matrix products, arithmetic and copies ran while one was open for 17% of the time, Pallas kernels for 0%

profile of v3, /device:TPU:0, one launch (start us, length us, event | category | flops | bytes accessed | tf_op | source)
XLA Modules:
  0.0 627.0 jit_solution(18413939853052504586)
XLA Ops:
  10.7 7.3 %all-to-all-start = ((s32[32,1,2]{2,1,0:T(1,128)}), s32[32,1,2]{2,1,0:T(1,128)S(1)}, u32[]{:S(2)}, u32[]{:S(2)}) async-start(s32[32,1,2]{2,1,0:T(1,128)} %bitcast.9), calls=%async_computation | async-start | bytes 32768 | tf_op jit(solution)/shard_map/all_to_all | solution.py:108
  18.0 2.9 reshape_squeeze.3
  25.3 5.3 scatter_fusion
  30.7 5.8 all-to-all-start.1
  39.3 87.7 %all-to-all-done.1 = f32[32,2,128,128]{3,2,1,0:T(8,128)} async-done(((f32[32,2,128,128]{3,2,1,0:T(8,128)}), f32[32,2,128,128]{3,2,1,0:T(8,128)}, u32[]{:S(2)}, u32[]{:S(2)}) %all-to-all-start.1) | async-done | bytes 4194336 | tf_op jit(solution)/shard_map/all_to_all | solution.py:105
  127.0 4.9 broadcast_in_dim.154
  131.9 13.6 %scatter_fusion.1 = f32[145,128,128]{2,1,0:T(8,128)} fusion(f32[145,128,128]{2,1,0:T(8,128)} %broadcast_in_dim.154, s32[64]{0:T(128)S(1)} %fusion.48, f32[64,128,128]{2,1,0:T(8,128)} %bitcast.14), kind=kCustom, calls=%fused_computation.2 | custom fusion | flops 1048576 | bytes 12583168 | tf_op jit(solution)/shard_map/scatter-add | solution.py:59
  145.5 8.8 %slice.101 = f32[144,128,128]{2,1,0:T(8,128)} slice(f32[145,128,128]{2,1,0:T(8,128)} %scatter_fusion.1), slice={[0:144], [0:128], [0:128]} | slice | bytes 18874368 | tf_op jit(solution)/shard_map/slice | solution.py:60
  154.3 12.6 %copy.90 = f32[12,128,12,128]{1,0,3,2:T(8,128)} copy(f32[12,128,12,128]{3,1,2,0:T(8,128)} %bitcast.84) | data formatting | bytes 18874368 | tf_op jit(solution)/shard_map/reshape | solution.py:62
  167.0 9.0 %bitcast_add_fusion = f32[1536,1536]{0,1:T(8,128)S(1)} fusion(f32[192,8,12,128]{3,2,1,0:T(8,128)} %bitcast.83, f32[1536]{0:T(1024)S(1)} %fusion.45, s32[1536]{0:T(1024)S(1)} %iota_add_fusion.1, s32[1536]{0:T(1024)S(1)} %get-tuple-element.36), kind=kLoop, calls=%fused_computation.7 | loop fusion | flops 7077888 | bytes 18892800 | tf_op jit(solution)/shard_map/add | solution.py:114
  176.0 3.7 copy-done.2
  187.6 3.9 collective-permute-start.2
  193.3 16.7 %collective-permute-done.2 = f32[256,768]{0,1:T(8,128)} collective-permute-done((f32[256,768]{0,1:T(8,128)}, f32[256,768]{0,1:T(8,128)}, u32[]{:S(2)}, u32[]{:S(2)}) %collective-permute-start.2) | collective-permute-done | bytes 786464 | tf_op jit(solution)/shard_map/ppermute | solution.py:29
  214.8 50.0 %collective-permute-done.3 = f32[256,768]{0,1:T(8,128)} collective-permute-done((f32[256,768]{0,1:T(8,128)S(1)}, f32[256,768]{0,1:T(8,128)}, u32[]{:S(2)}, u32[]{:S(2)}) %collective-permute-start.3) | collective-permute-done | bytes 786464 | tf_op jit(solution)/shard_map/ppermute | solution.py:29
  267.8 6.3 %all-reduce.5.cloned.1.call-done = f32[256,768]{0,1:T(8,128)} async-done(((f32[256,768]{0,1:T(8,128)}), f32[256,768]{0,1:T(8,128)}) %all-reduce.5.cloned.1.call-update) | async-done | bytes 786448 | tf_op jit(solution)/shard_map/psum | solution.py:18
  274.1 3.2 fusion.5
  277.3 3.8 fusion.21
  281.1 2.9 fusion.4
  290.1 16.2 %collective-permute-done.6 = f32[256,768]{0,1:T(8,128)} collective-permute-done((f32[256,768]{0,1:T(8,128)}, f32[256,768]{0,1:T(8,128)}, u32[]{:S(2)}, u32[]{:S(2)}) %collective-permute-start.6) | collective-permute-done | bytes 786464 | tf_op jit(solution)/shard_map/ppermute | solution.py:29
  306.3 2.7 slice_select_fusion.2
  310.5 2.8 broadcast_select_fusion.4
  313.9 12.9 %subtract_select_fusion.3 = f32[1536,1536]{0,1:T(8,128)} fusion(f32[1536,1536]{0,1:T(8,128)} %copy-done.2, f32[1536,256]{0,1:T(8,128)S(1)} %broadcast_select_fusion.7, pred[1536]{0:T(1024)(128)(4,1)S(1)} %get-tuple-element.32, pred[1536]{0:T(1024)(128)(4,1)S(1)} %get-tuple-element.31, f32[256,768]{0,1:T(8,128)S(1)} %broadcast_select_fusion.16, ...), kind=kOutput, calls=%fused_computation.6 | convolution fusion | flops 7255228416 | bytes 22023168 | tf_op jit(solution)/shard_map/dot_general | solution.py:188
  326.8 2.9 select_dynamic-update-slice_fusion.2
  330.0 28.9 %collective-permute-done.7 = f32[256,768]{0,1:T(8,128)} collective-permute-done((f32[256,768]{0,1:T(8,128)}, f32[256,768]{0,1:T(8,128)}, u32[]{:S(2)}, u32[]{:S(2)}) %collective-permute-start.7) | collective-permute-done | bytes 786464 | tf_op jit(solution)/shard_map/ppermute | solution.py:29
  361.8 18.7 %all-reduce.7.cloned.1.call-done = f32[256,768]{0,1:T(8,128)} async-done(((f32[256,768]{0,1:T(8,128)}), f32[256,768]{0,1:T(8,128)}) %all-reduce.7.cloned.1.call-update) | async-done | bytes 786448 | tf_op jit(solution)/shard_map/psum | solution.py:18
  380.5 3.1 fusion.3
  383.6 3.8 fusion.19
  387.4 2.9 fusion.2
  395.5 17.1 %collective-permute-done.10 = f32[256,768]{0,1:T(8,128)} collective-permute-done((f32[256,768]{0,1:T(8,128)}, f32[256,768]{0,1:T(8,128)}, u32[]{:S(2)}, u32[]{:S(2)}) %collective-permute-start.10) | collective-permute-done | bytes 786464 | tf_op jit(solution)/shard_map/ppermute | solution.py:29
  412.6 2.7 slice_select_fusion.1
  416.8 2.8 broadcast_select_fusion.2
  421.0 12.9 %subtract_select_fusion.2 = f32[1536,1536]{0,1:T(8,128)} fusion(f32[1536,1536]{0,1:T(8,128)} %select_dynamic-update-slice_fusion.2, f32[1536,256]{0,1:T(8,128)S(1)} %broadcast_select_fusion.5, pred[1536]{0:T(1024)(128)(4,1)S(1)} %get-tuple-element.10, pred[1536]{0:T(1024)(128)(4,1)S(1)} %get-tuple-element.9, f32[256,768]{0,1:T(8,128)S(1)} %broadcast_select_fusion.14, ...), kind=kOutput, calls=%fused_computation.5 | convolution fusion | flops 7255228416 | bytes 22023168 | tf_op jit(solution)/shard_map/dot_general | solution.py:188
  434.0 2.9 select_dynamic-update-slice_fusion.1
  437.2 28.1 %collective-permute-done.11 = f32[256,768]{0,1:T(8,128)} collective-permute-done((f32[256,768]{0,1:T(8,128)}, f32[256,768]{0,1:T(8,128)}, u32[]{:S(2)}, u32[]{:S(2)}) %collective-permute-start.11) | collective-permute-done | bytes 786464 | tf_op jit(solution)/shard_map/ppermute | solution.py:29
  468.4 18.3 %all-reduce.9.cloned.1.call-done = f32[256,768]{0,1:T(8,128)} async-done(((f32[256,768]{0,1:T(8,128)}), f32[256,768]{0,1:T(8,128)}) %all-reduce.9.cloned.1.call-update) | async-done | bytes 786448 | tf_op jit(solution)/shard_map/psum | solution.py:18
  486.7 3.2 fusion.1
  489.9 3.8 fusion.17
  493.7 2.9 fusion
  500.5 17.3 %collective-permute-done.14 = f32[256,768]{0,1:T(8,128)S(1)} collective-permute-done((f32[256,768]{0,1:T(8,128)S(1)}, f32[256,768]{0,1:T(8,128)S(1)}, u32[]{:S(2)}, u32[]{:S(2)}) %collective-permute-start.14) | collective-permute-done | bytes 786464 | tf_op jit(solution)/shard_map/ppermute | solution.py:29
  517.8 2.8 slice_select_fusion
  525.2 13.2 %subtract_select_fusion.1 = f32[1536,1536]{0,1:T(8,128)} fusion(f32[1536,1536]{0,1:T(8,128)} %select_dynamic-update-slice_fusion.1, f32[1536,256]{0,1:T(8,128)S(1)} %broadcast_select_fusion.3, pred[1536]{0:T(1024)(128)(4,1)S(1)} %get-tuple-element.8, pred[1536]{0:T(1024)(128)(4,1)S(1)} %get-tuple-element.7, f32[256,768]{0,1:T(8,128)S(1)} %copy-done.4, ...), kind=kOutput, calls=%fused_computation.4 | convolution fusion | flops 7255228416 | bytes 22023168 | tf_op jit(solution)/shard_map/dot_general | solution.py:188
  538.5 2.9 select_dynamic-update-slice_fusion
  541.3 29.1 %collective-permute-done.15 = f32[256,768]{0,1:T(8,128)} collective-permute-done((f32[256,768]{0,1:T(8,128)}, f32[256,768]{0,1:T(8,128)}, u32[]{:S(2)}, u32[]{:S(2)}) %collective-permute-start.15) | collective-permute-done | bytes 786464 | tf_op jit(solution)/shard_map/ppermute | solution.py:29
  571.7 20.0 %all-reduce.11.cloned.1.call-done = f32[256,768]{0,1:T(8,128)} async-done(((f32[256,768]{0,1:T(8,128)}), f32[256,768]{0,1:T(8,128)}) %all-reduce.11.cloned.1.call-update) | async-done | bytes 786448 | tf_op jit(solution)/shard_map/psum | solution.py:18
  591.7 12.1 %subtract_select_fusion = f32[1536,1536]{0,1:T(8,128)S(1)} fusion(f32[1536,1536]{0,1:T(8,128)} %select_dynamic-update-slice_fusion, pred[1536]{0:T(1024)(128)(4,1)S(1)} %get-tuple-element.6, pred[1536]{0:T(1024)(128)(4,1)S(1)} %get-tuple-element.5, f32[256,768]{0,1:T(8,128)S(1)} %broadcast_select_fusion.10, f32[256,768]{0,1:T(8,128)} %all-reduce.11.cloned.1.call-done, ...), kind=kOutput, calls=%fused_computation.3 | convolution fusion | flops 7255621632 | bytes 23596032 | tf_op jit(solution)/shard_map/dot_general | solution.py:188
  603.8 3.6 copy.103
  607.5 2.9 bitcast_dynamic-update-slice_fusion
  610.4 9.6 %copy.79 = f32[1,1536,1536]{2,1,0:T(8,128)} copy(f32[1,1536,1536]{1,2,0:T(8,128)} %bitcast_dynamic-update-slice_fusion) | data formatting | bytes 18874368 | tf_op jit(solution)/shard_map/dynamic_update_slice | solution.py:203
  (120 shorter events, 53.6 us)
Async XLA Ops:
  6.5 31.3 %copy-start = (f32[1,6144]{1,0:T(1,128)S(1)}, f32[1,6144]{1,0:T(1,128)}, u32[]{:S(2)}) copy-start(f32[1,6144]{1,0:T(1,128)} %param.11) | copy-start | bytes 73732
  10.7 19.9 %all-to-all-start = ((s32[32,1,2]{2,1,0:T(1,128)}), s32[32,1,2]{2,1,0:T(1,128)S(1)}, u32[]{:S(2)}, u32[]{:S(2)}) async-start(s32[32,1,2]{2,1,0:T(1,128)} %bitcast.9), calls=%async_computation | async-start | bytes 32768 | tf_op jit(solution)/shard_map/all_to_all | solution.py:108
  30.7 5.9 copy-start.14
  30.7 96.3 %all-to-all-start.1 = ((f32[32,2,128,128]{3,2,1,0:T(8,128)}), f32[32,2,128,128]{3,2,1,0:T(8,128)}, u32[]{:S(2)}, u32[]{:S(2)}) async-start(f32[32,2,128,128]{3,2,1,0:T(8,128)} %bitcast.85), calls=%async_computation.1 | async-start | bytes 8388608 | tf_op jit(solution)/shard_map/all_to_all | solution.py:105
  36.5 237.6 %all-reduce.5.cloned.1.call-start = ((), (), s32[]{:S(2)}) async-start(), calls=%async_computation.2 | async-start | bytes 1572864 | tf_op jit(solution)/shard_map/psum | solution.py:18
  176.0 3.7 copy-start.2
  182.2 9.3 %collective-permute-start = (f32[1536,256]{0,1:T(8,128)S(1)}, f32[1536,256]{0,1:T(8,128)}, u32[]{:S(2)}, u32[]{:S(2)}) collective-permute-start(f32[1536,256]{0,1:T(8,128)S(1)} %fusion.9), channel_id=1, source_target_pairs={{0,4},{4,0},{8,12},{12,8},{1,5},{5,1},{9,13},{13,9},{2,6},{6,2},{1... | collective-permute-start | bytes 4718600 | tf_op jit(solution)/shard_map/ppermute | solution.py:29
  187.6 22.4 %collective-permute-start.2 = (f32[256,768]{0,1:T(8,128)}, f32[256,768]{0,1:T(8,128)}, u32[]{:S(2)}, u32[]{:S(2)}) collective-permute-start(f32[256,768]{0,1:T(8,128)} %get-tuple-element.16), channel_id=1, source_target_pairs={{0,1},{1,0},{2,3},{3,2},{4,5},{5,4},{6,7},{7,6},{8,9},{9,8},{10,11... | collective-permute-start | bytes 2359304 | tf_op jit(solution)/shard_map/ppermute | solution.py:29
  193.2 21.4 %copy-start.12 = (f32[1536,256]{0,1:T(8,128)}, f32[1536,256]{0,1:T(8,128)S(1)}, u32[]{:S(2)}) copy-start(f32[1536,256]{0,1:T(8,128)S(1)} %broadcast_select_fusion.6) | copy-start | bytes 4718596
  193.2 72.9 %collective-permute-start.1 = (f32[1536,256]{0,1:T(8,128)S(1)}, f32[1536,256]{0,1:T(8,128)}, u32[]{:S(2)}, u32[]{:S(2)}) collective-permute-start(f32[1536,256]{0,1:T(8,128)S(1)} %broadcast_select_fusion.6), channel_id=1, source_target_pairs={{0,8},{4,12},{8,0},{12,4},{1,9},{5,13},{9,1},{13,5},{2,10},{6,14},... | collective-permute-start | bytes 4718600 | tf_op jit(solution)/shard_map/ppermute | solution.py:29
  211.2 53.6 %collective-permute-start.3 = (f32[256,768]{0,1:T(8,128)S(1)}, f32[256,768]{0,1:T(8,128)}, u32[]{:S(2)}, u32[]{:S(2)}) collective-permute-start(f32[256,768]{0,1:T(8,128)S(1)} %broadcast_select_fusion.15), channel_id=1, source_target_pairs={{0,2},{1,3},{2,0},{3,1},{4,6},{5,7},{6,4},{7,5},{8,10},{9,11},{10,... | collective-permute-start | bytes 2359304 | tf_op jit(solution)/shard_map/ppermute | solution.py:29
  214.6 165.9 %all-reduce.7.cloned.1.call-start = ((), (), s32[]{:S(2)}) async-start(), calls=%async_computation.3 | async-start | bytes 1572864 | tf_op jit(solution)/shard_map/psum | solution.py:18
  214.8 51.3 %copy-start.13 = (f32[1536,256]{0,1:T(8,128)S(1)}, f32[1536,256]{0,1:T(8,128)}, u32[]{:S(2)}) copy-start(f32[1536,256]{0,1:T(8,128)} %copy-done.12) | copy-start | bytes 4718596
  277.3 3.8 copy-start.8
  281.1 29.5 %collective-permute-start.4 = (f32[1536,256]{0,1:T(8,128)}, f32[1536,256]{0,1:T(8,128)}, u32[]{:S(2)}, u32[]{:S(2)}) collective-permute-start(f32[1536,256]{0,1:T(8,128)} %fusion.21), channel_id=1, source_target_pairs={{0,4},{4,0},{8,12},{12,8},{1,5},{5,1},{9,13},{13,9},{2,6},{6,2},{1... | collective-permute-start | bytes 4718600 | tf_op jit(solution)/shard_map/ppermute | solution.py:29
  284.0 1.1 copy-start.5
  286.1 20.2 %collective-permute-start.6 = (f32[256,768]{0,1:T(8,128)}, f32[256,768]{0,1:T(8,128)}, u32[]{:S(2)}, u32[]{:S(2)}) collective-permute-start(f32[256,768]{0,1:T(8,128)} %slice.103), channel_id=1, source_target_pairs={{0,1},{1,0},{2,3},{3,2},{4,5},{5,4},{6,7},{7,6},{8,9},{9,8},{10,11... | collective-permute-start | bytes 2359304 | tf_op jit(solution)/shard_map/ppermute | solution.py:29
  309.0 49.9 %collective-permute-start.7 = (f32[256,768]{0,1:T(8,128)}, f32[256,768]{0,1:T(8,128)}, u32[]{:S(2)}, u32[]{:S(2)}) collective-permute-start(f32[256,768]{0,1:T(8,128)} %get-tuple-element.22), channel_id=1, source_target_pairs={{0,2},{1,3},{2,0},{3,1},{4,6},{5,7},{6,4},{7,5},{8,10},{9,11},{10,... | collective-permute-start | bytes 2359304 | tf_op jit(solution)/shard_map/ppermute | solution.py:29
  313.3 46.8 %collective-permute-start.5 = (f32[1536,256]{0,1:T(8,128)}, f32[1536,256]{0,1:T(8,128)}, u32[]{:S(2)}, u32[]{:S(2)}) collective-permute-start(f32[1536,256]{0,1:T(8,128)} %broadcast_select_fusion.4), channel_id=1, source_target_pairs={{0,8},{4,12},{8,0},{12,4},{1,9},{5,13},{9,1},{13,5},{2,10},{6,14},... | collective-permute-start | bytes 4718600 | tf_op jit(solution)/shard_map/ppermute | solution.py:29
  329.7 156.9 %all-reduce.9.cloned.1.call-start = ((), (), s32[]{:S(2)}) async-start(), calls=%async_computation.4 | async-start | bytes 1572864 | tf_op jit(solution)/shard_map/psum | solution.py:18
  383.6 3.8 copy-start.9
  387.4 29.4 %collective-permute-start.8 = (f32[1536,256]{0,1:T(8,128)}, f32[1536,256]{0,1:T(8,128)}, u32[]{:S(2)}, u32[]{:S(2)}) collective-permute-start(f32[1536,256]{0,1:T(8,128)} %fusion.19), channel_id=1, source_target_pairs={{0,4},{4,0},{8,12},{12,8},{1,5},{5,1},{9,13},{13,9},{2,6},{6,2},{1... | collective-permute-start | bytes 4718600 | tf_op jit(solution)/shard_map/ppermute | solution.py:29
  390.3 1.1 copy-start.6
  392.4 20.3 %collective-permute-start.10 = (f32[256,768]{0,1:T(8,128)}, f32[256,768]{0,1:T(8,128)}, u32[]{:S(2)}, u32[]{:S(2)}) collective-permute-start(f32[256,768]{0,1:T(8,128)} %slice.105), channel_id=1, source_target_pairs={{0,1},{1,0},{2,3},{3,2},{4,5},{5,4},{6,7},{7,6},{8,9},{9,8},{10,11... | collective-permute-start | bytes 2359304 | tf_op jit(solution)/shard_map/ppermute | solution.py:29
  415.3 49.9 %collective-permute-start.11 = (f32[256,768]{0,1:T(8,128)}, f32[256,768]{0,1:T(8,128)}, u32[]{:S(2)}, u32[]{:S(2)}) collective-permute-start(f32[256,768]{0,1:T(8,128)} %get-tuple-element.20), channel_id=1, source_target_pairs={{0,2},{1,3},{2,0},{3,1},{4,6},{5,7},{6,4},{7,5},{8,10},{9,11},{10,... | collective-permute-start | bytes 2359304 | tf_op jit(solution)/shard_map/ppermute | solution.py:29
  419.6 46.9 %collective-permute-start.9 = (f32[1536,256]{0,1:T(8,128)}, f32[1536,256]{0,1:T(8,128)}, u32[]{:S(2)}, u32[]{:S(2)}) collective-permute-start(f32[1536,256]{0,1:T(8,128)} %broadcast_select_fusion.2), channel_id=1, source_target_pairs={{0,8},{4,12},{8,0},{12,4},{1,9},{5,13},{9,1},{13,5},{2,10},{6,14},... | collective-permute-start | bytes 4718600 | tf_op jit(solution)/shard_map/ppermute | solution.py:29
  436.9 154.8 %all-reduce.11.cloned.1.call-start = ((), (), s32[]{:S(2)}) async-start(), calls=%async_computation.5 | async-start | bytes 1572864 | tf_op jit(solution)/shard_map/psum | solution.py:18
  466.5 27.2 %copy-start.3 = (f32[256,768]{0,1:T(8,128)}, f32[256,768]{0,1:T(8,128)S(1)}, u32[]{:S(2)}) copy-start(f32[256,768]{0,1:T(8,128)S(1)} %broadcast_select_fusion.12) | copy-start | bytes 2359300
  489.9 3.8 copy-start.10
  493.7 28.4 %collective-permute-start.12 = (f32[1536,256]{0,1:T(8,128)}, f32[1536,256]{0,1:T(8,128)}, u32[]{:S(2)}, u32[]{:S(2)}) collective-permute-start(f32[1536,256]{0,1:T(8,128)} %fusion.17), channel_id=1, source_target_pairs={{0,4},{4,0},{8,12},{12,8},{1,5},{5,1},{9,13},{13,9},{2,6},{6,2},{1... | collective-permute-start | bytes 4718600 | tf_op jit(solution)/shard_map/ppermute | solution.py:29
  496.6 1.1 copy-start.7
  497.8 20.0 %collective-permute-start.14 = (f32[256,768]{0,1:T(8,128)S(1)}, f32[256,768]{0,1:T(8,128)S(1)}, u32[]{:S(2)}, u32[]{:S(2)}) collective-permute-start(f32[256,768]{0,1:T(8,128)S(1)} %slice.107), channel_id=1, source_target_pairs={{0,1},{1,0},{2,3},{3,2},{4,5},{5,4},{6,7},{7,6},{8,9},{9,8},{10,11... | collective-permute-start | bytes 2359304 | tf_op jit(solution)/shard_map/ppermute | solution.py:29
  520.6 4.6 copy-start.4
  520.6 4.6 copy-start.11
  520.6 49.9 %collective-permute-start.15 = (f32[256,768]{0,1:T(8,128)}, f32[256,768]{0,1:T(8,128)}, u32[]{:S(2)}, u32[]{:S(2)}) collective-permute-start(f32[256,768]{0,1:T(8,128)} %get-tuple-element.18), channel_id=1, source_target_pairs={{0,2},{1,3},{2,0},{3,1},{4,6},{5,7},{6,4},{7,5},{8,10},{9,11},{10,... | collective-permute-start | bytes 2359304 | tf_op jit(solution)/shard_map/ppermute | solution.py:29
  523.7 68.0 %collective-permute-start.13 = (f32[1536,256]{0,1:T(8,128)S(1)}, f32[1536,256]{0,1:T(8,128)}, u32[]{:S(2)}, u32[]{:S(2)}) collective-permute-start(f32[1536,256]{0,1:T(8,128)S(1)} %broadcast_select_fusion), channel_id=1, source_target_pairs={{0,8},{4,12},{8,0},{12,4},{1,9},{5,13},{9,1},{13,5},{2,10},{6,14},... | collective-permute-start | bytes 4718600 | tf_op jit(solution)/shard_map/ppermute | solution.py:29
  610.4 9.6 %copy-start.1 = (f32[1,6144]{1,0:T(1,128)S(1)}, f32[1,6144]{1,0:T(1,128)}, u32[]{:S(2)}) copy-start(f32[1,6144]{1,0:T(1,128)} %param.11) | copy-start | bytes 73732
Sparse Core Ops, SparseCore 0:
  214.7 59.3 all-reduce.4
  329.8 50.5 all-reduce.6
  437.0 49.6 all-reduce.8
  538.6 53.0 all-reduce.10

commit v4 on v1

--- a/solution.py
+++ b/solution.py
@@ -53,13 +53,16 @@
     )
 
 
-def scatter_tiles(payload, labels, row_tiles, col_tiles):
+def scatter_tiles(payload, labels, base, row_tiles, col_tiles):
     tile_side = payload.shape[-1]
-    tile_grid = jnp.zeros((row_tiles * col_tiles + 1, tile_side, tile_side), jnp.float32)
-    tile_grid = tile_grid.at[labels.reshape(-1)].add(payload.reshape(-1, tile_side, tile_side))
-    tile_grid = tile_grid[: row_tiles * col_tiles]
-    tile_grid = tile_grid.reshape(row_tiles, col_tiles, tile_side, tile_side).transpose(0, 2, 1, 3)
-    return tile_grid.reshape(row_tiles * tile_side, col_tiles * tile_side)
+    spots = labels.reshape(-1)
+    tile_rows = spots // col_tiles
+    tile_cols = spots % col_tiles
+    grid = base.reshape(row_tiles, tile_side, col_tiles, tile_side)
+    grid = grid.at[tile_rows, :, tile_cols, :].add(
+        payload.reshape(-1, tile_side, tile_side), mode="drop"
+    )
+    return grid.reshape(row_tiles * tile_side, col_tiles * tile_side)
 
 
 def body(cbs, row_map, col_map, child_size, front_diag, panel_order, pivot_inverse):
@@ -107,11 +110,11 @@
         ),
         lax.all_to_all(labels, ("front", "column", "row"), split_axis=0, concat_axis=0, tiled=True),
     )
-    matrix = scatter_tiles(arrived, arrived_labels, row_tiles, col_tiles)
     row_glob = row_id * local_rows + jnp.arange(local_rows, dtype=jnp.int32)
     col_glob = col_id * local_cols + jnp.arange(local_cols, dtype=jnp.int32)
     diag_part = lax.dynamic_slice_in_dim(front_diag[0], row_id * local_rows, local_rows)
-    matrix = matrix + jnp.where(row_glob[:, None] == col_glob[None, :], diag_part[:, None], 0.0)
+    diag_block = jnp.where(row_glob[:, None] == col_glob[None, :], diag_part[:, None], 0.0)
+    matrix = scatter_tiles(arrived, arrived_labels, diag_block, row_tiles, col_tiles)
     order_row = panel_order[0]
     inverses = pivot_inverse[0]
     panel_rows = local_rows // PANEL

time: 537 us -> 535 us (level)
    scatter-add x0 -> x1, local copies, waits for them, and re-layouts: none -> 14.5 us  [scatter_tiles(): grid.at[tile_rows, :, tile_cols, :]]
    transpose x1 -> x0, local copies, waits for them, and re-layouts: 9.92 us -> none  [scatter_tiles(): tile_grid.reshape(row_tiles, col_tiles, tile_side, tile_side)]
    unnamed x15 -> x16, local copies, waits for them, and re-layouts: 7.51 us -> 16.8 us
    slice x1 -> x0, local copies, waits for them, and re-layouts: 8.8 us -> none  [scatter_tiles(): tile_grid = tile_grid[:row_tiles * col_tiles]]
  transfers between devices with their start and end apart: 14 -> 14, of which waited for: 11 -> 11; matrix products, arithmetic and copies ran while one was open for 16% -> 17% of each run, Pallas kernels for 0% -> 0%
where the time goes in v4:
time: 535 us; the launch traced here: 530 us
  waiting for transfers between devices  304 us (57%)
  matrix products  85.9 us (16%)
  other arithmetic  49.6 us (9%)
  local copies, waits for them, and re-layouts  47 us (9%)
  between operations  21.9 us (4%)
  starting transfers between devices  21.2 us (4%)
    psum x4, waiting for transfers between devices, broadcast(): return lax.psum(block, axis)  155 us
    all_to_all x1, waiting for transfers between devices, body(): lax.all_to_all(payload, ('front', 'column', 'row'), split_axis=0, concat_...  84.1 us
    ppermute x8, waiting for transfers between devices, exchange_broadcast(): received = lax.ppermute(block, axis, partner)  65.7 us
    dot_general x4, matrix products, body(): jnp.dot(left_strip, top_strip, precision=HIGHEST, preferred_element_type=...  51.5 us
    unnamed x16, local copies, waits for them, and re-layouts  16.8 us
    scatter-add x1, local copies, waits for them, and re-layouts, scatter_tiles(): grid.at[tile_rows, :, tile_cols, :]  14.5 us
    scatter-add x1, other arithmetic, scatter_tiles(): grid.at[tile_rows, :, tile_cols, :]  13.7 us
    dot_general x4, matrix products, share_strips(): jnp.dot(col_strip, inverses[step_index], precision=HIGHEST, preferred_ele...  13.2 us
  transfers between devices with their start and end apart: 14, of which 11 were waited for; matrix products, arithmetic and copies ran while one was open for 17% of the time, Pallas kernels for 0%

profile of v4, /device:TPU:0, one launch (start us, length us, event | category | flops | bytes accessed | tf_op | source)
XLA Modules:
  0.0 530.0 jit_solution(14205873276315905286)
XLA Ops:
  10.7 7.3 %all-to-all-start = ((s32[32,1,2]{2,1,0:T(1,128)}), s32[32,1,2]{2,1,0:T(1,128)S(1)}, u32[]{:S(2)}, u32[]{:S(2)}) async-start(s32[32,1,2]{2,1,0:T(1,128)} %bitcast.9), calls=%async_computation | async-start | bytes 32768 | tf_op jit(solution)/shard_map/all_to_all | solution.py:111
  18.0 2.9 reshape_squeeze.3
  20.9 1.9 copy.16
  22.8 2.5 broadcast_in_dim.159
  25.3 5.4 %scatter_fusion = f32[64,128,128]{2,1,0:T(8,128)} fusion(f32[64,128,128]{2,1,0:T(8,128)} %broadcast_in_dim.159, s32[32]{0:T(128)S(1)} %fusion.49, f32[32,128,128]{2,1,0:T(8,128)S(1)} %bitcast.94), kind=kCustom, calls=%fused_computation.1 | custom fusion | bytes 6291584 | tf_op jit(solution)/shard_map/scatter | solution.py:44
  30.7 5.9 %all-to-all-start.1 = ((f32[32,2,128,128]{3,2,1,0:T(8,128)}), f32[32,2,128,128]{3,2,1,0:T(8,128)}, u32[]{:S(2)}, u32[]{:S(2)}) async-start(f32[32,2,128,128]{3,2,1,0:T(8,128)} %bitcast.93), calls=%async_computation.1 | async-start | bytes 8388608 | tf_op jit(solution)/shard_map/all_to_all | solution.py:108
  38.0 4.4 compare_select_fusion
  43.0 84.1 %all-to-all-done.1 = f32[32,2,128,128]{3,2,1,0:T(8,128)} async-done(((f32[32,2,128,128]{3,2,1,0:T(8,128)}), f32[32,2,128,128]{3,2,1,0:T(8,128)}, u32[]{:S(2)}, u32[]{:S(2)}) %all-to-all-start.1) | async-done | bytes 4194336 | tf_op jit(solution)/shard_map/all_to_all | solution.py:108
  127.1 13.7 %scatter_fusion.1 = f32[12,128,12,128]{3,1,2,0:T(8,128)} fusion(f32[12,128,12,128]{3,1,2,0:T(8,128)} %compare_select_fusion, s32[64]{0:T(128)S(1)} %fusion.48, f32[64,128,128]{2,1,0:T(8,128)} %bitcast.14), kind=kCustom, calls=%fused_computation.2 | custom fusion | flops 1048576 | bytes 12583424 | tf_op jit(solution)/shard_map/scatter-add | solution.py:62
  140.8 14.5 %copy.17 = f32[12,128,12,128]{3,2,1,0:T(8,128)} copy(f32[12,128,12,128]{3,1,2,0:T(8,128)} %scatter_fusion.1) | data formatting | bytes 18874368 | tf_op jit(solution)/shard_map/scatter-add | solution.py:62
  155.3 9.3 %copy.20 = f32[192,8,12,128]{3,1,2,0:T(8,128)S(1)} copy(f32[192,8,12,128]{3,2,1,0:T(8,128)} %bitcast.91) | data formatting | bytes 18874368
  164.6 3.7 copy-done.2
  168.3 2.7 fusion.9
  171.0 1.8 collective-permute-start
  174.1 1.9 collective-permute-done
  177.8 2.6 dynamic-slice_select_fusion
  181.9 31.0 %collective-permute-done.1 = f32[1536,256]{1,0:T(8,128)} collective-permute-done((f32[1536,256]{1,0:T(8,128)S(1)}, f32[1536,256]{1,0:T(8,128)}, u32[]{:S(2)}, u32[]{:S(2)}) %collective-permute-start.1) | collective-permute-done | bytes 1572896 | tf_op jit(solution)/shard_map/ppermute | solution.py:29
  213.0 1.7 broadcast_select_fusion.7
  214.7 36.8 %all-reduce.5.cloned.1.call-done = f32[256,1536]{1,0:T(8,128)} async-done(((f32[256,1536]{1,0:T(8,128)}), f32[256,1536]{1,0:T(8,128)}) %all-reduce.5.cloned.1.call-update) | async-done | bytes 1572880 | tf_op jit(solution)/shard_map/psum | solution.py:18
  251.5 2.9 fusion.8
  254.4 3.5 fusion.15
  261.6 2.8 broadcast_select_fusion.4
  266.0 4.1 fusion.7
  270.2 12.9 %subtract_select_fusion.3 = f32[1536,1536]{1,0:T(8,128)} fusion(f32[1536,1536]{1,0:T(8,128)} %bitcast.90, f32[1536,256]{1,0:T(8,128)S(1)} %broadcast_select_fusion.7, f32[256,1536]{1,0:T(8,128)S(1)} %copy-done.3, pred[1536]{0:T(1024)(128)(4,1)S(1)} %broadcast_compare_fusion, pred[1536]{0:T(1024)(128)(4,1)S(1)} %broadcast_compare_fusion.1), kind=kOutput, calls=%fused_computation.6 | convolution fusion | flops 7254835200 | bytes 22023168 | tf_op jit(solution)/shard_map/dot_general | solution.py:184
  283.1 2.9 select_dynamic-update-slice_fusion.2
  286.0 15.5 %collective-permute-done.3 = f32[1536,256]{1,0:T(8,128)} collective-permute-done((f32[1536,256]{1,0:T(8,128)}, f32[1536,256]{1,0:T(8,128)}, u32[]{:S(2)}, u32[]{:S(2)}) %collective-permute-start.3) | collective-permute-done | bytes 1572896 | tf_op jit(solution)/shard_map/ppermute | solution.py:29
  301.5 1.6 broadcast_select_fusion.5
  303.1 34.4 %all-reduce.7.cloned.1.call-done = f32[256,1536]{1,0:T(8,128)} async-done(((f32[256,1536]{1,0:T(8,128)}), f32[256,1536]{1,0:T(8,128)}) %all-reduce.7.cloned.1.call-update) | async-done | bytes 1572880 | tf_op jit(solution)/shard_map/psum | solution.py:18
  337.6 2.9 fusion.5
  340.5 3.5 fusion.13
  346.2 1.5 collective-permute-done.4
  347.8 2.7 broadcast_select_fusion.2
  352.0 4.1 fusion.4
  356.2 12.6 %subtract_select_fusion.2 = f32[1536,1536]{1,0:T(8,128)} fusion(f32[1536,1536]{1,0:T(8,128)} %select_dynamic-update-slice_fusion.2, f32[1536,256]{1,0:T(8,128)S(1)} %broadcast_select_fusion.5, f32[256,1536]{1,0:T(8,128)S(1)} %copy-done.4, pred[1536]{0:T(1024)(128)(4,1)S(1)} %get-tuple-element.12, pred[1536]{0:T(1024)(128)(4,1)S(1)} %get-tuple-element.11), kind=kOutput, calls=%fused_computation.5 | convolution fusion | flops 7254835200 | bytes 22023168 | tf_op jit(solution)/shard_map/dot_general | solution.py:184
  368.8 2.9 select_dynamic-update-slice_fusion.1
  371.7 15.6 %collective-permute-done.5 = f32[1536,256]{1,0:T(8,128)} collective-permute-done((f32[1536,256]{1,0:T(8,128)}, f32[1536,256]{1,0:T(8,128)}, u32[]{:S(2)}, u32[]{:S(2)}) %collective-permute-start.5) | collective-permute-done | bytes 1572896 | tf_op jit(solution)/shard_map/ppermute | solution.py:29
  387.3 1.6 broadcast_select_fusion.3
  388.9 34.7 %all-reduce.9.cloned.1.call-done = f32[256,1536]{1,0:T(8,128)} async-done(((f32[256,1536]{1,0:T(8,128)}), f32[256,1536]{1,0:T(8,128)}) %all-reduce.9.cloned.1.call-update) | async-done | bytes 1572880 | tf_op jit(solution)/shard_map/psum | solution.py:18
  423.5 2.9 fusion.2
  426.5 3.6 fusion.11
  431.4 4.1 fusion.1
  435.5 1.6 broadcast_select_fusion
  438.9 13.5 %subtract_select_fusion.1 = f32[1536,1536]{1,0:T(8,128)} fusion(f32[1536,1536]{1,0:T(8,128)} %select_dynamic-update-slice_fusion.1, f32[1536,256]{1,0:T(8,128)S(1)} %broadcast_select_fusion.3, f32[256,1536]{1,0:T(8,128)} %all-reduce.9.cloned.1.call-done, pred[1536]{0:T(1024)(128)(4,1)S(1)} %get-tuple-element.10, pred[1536]{0:T(1024)(128)(4,1)S(1)} %get-tuple-element.9), kind=kOutput, calls=%fused_computation.4 | convolution fusion | flops 7254835200 | bytes 22023168 | tf_op jit(solution)/shard_map/dot_general | solution.py:184
  452.3 3.0 select_dynamic-update-slice_fusion
  455.3 48.7 %all-reduce.11.cloned.1.call-done = f32[256,1536]{1,0:T(8,128)} async-done(((f32[256,1536]{1,0:T(8,128)}), f32[256,1536]{1,0:T(8,128)}) %all-reduce.11.cloned.1.call-update) | async-done | bytes 1572880 | tf_op jit(solution)/shard_map/psum | solution.py:18
  504.0 12.5 %subtract_select_fusion = f32[1536,1536]{1,0:T(8,128)S(1)} fusion(f32[1536,1536]{1,0:T(8,128)} %select_dynamic-update-slice_fusion, f32[256,1536]{1,0:T(8,128)} %all-reduce.11.cloned.1.call-done, pred[1536]{0:T(1024)(128)(4,1)S(1)} %get-tuple-element.8, pred[1536]{0:T(1024)(128)(4,1)S(1)} %get-tuple-element.7, f32[1536,256]{1,0:T(8,128)} %collective-permute-done.7, ...), kind=kOutput, calls=%fused_computation.3 | convolution fusion | flops 7255228416 | bytes 23596032 | tf_op jit(solution)/shard_map/dot_general | solution.py:184
  516.5 3.7 copy.30
  520.3 2.9 bitcast_dynamic-update-slice_fusion
  (77 shorter events, 14.4 us)
Async XLA Ops:
  6.5 31.4 %copy-start = (f32[1,6144]{1,0:T(1,128)S(1)}, f32[1,6144]{1,0:T(1,128)}, u32[]{:S(2)}) copy-start(f32[1,6144]{1,0:T(1,128)} %param.11) | copy-start | bytes 73732
  10.7 20.0 %all-to-all-start = ((s32[32,1,2]{2,1,0:T(1,128)}), s32[32,1,2]{2,1,0:T(1,128)S(1)}, u32[]{:S(2)}, u32[]{:S(2)}) async-start(s32[32,1,2]{2,1,0:T(1,128)} %bitcast.9), calls=%async_computation | async-start | bytes 32768 | tf_op jit(solution)/shard_map/all_to_all | solution.py:111
  30.7 6.0 %copy-start.6 = (s32[1,4]{1,0:T(1,128)S(1)}, s32[1,4]{1,0:T(1,128)}, u32[]{:S(2)}) copy-start(s32[1,4]{1,0:T(1,128)} %param.12) | copy-start | bytes 52
  30.7 96.4 %all-to-all-start.1 = ((f32[32,2,128,128]{3,2,1,0:T(8,128)}), f32[32,2,128,128]{3,2,1,0:T(8,128)}, u32[]{:S(2)}, u32[]{:S(2)}) async-start(f32[32,2,128,128]{3,2,1,0:T(8,128)} %bitcast.93), calls=%async_computation.1 | async-start | bytes 8388608 | tf_op jit(solution)/shard_map/all_to_all | solution.py:108
  36.6 214.9 %all-reduce.5.cloned.1.call-start = ((), (), s32[]{:S(2)}) async-start(), calls=%async_computation.2 | async-start | bytes 3145728 | tf_op jit(solution)/shard_map/psum | solution.py:18
  164.6 3.7 copy-start.2
  171.0 5.0 collective-permute-start
  176.3 36.7 %collective-permute-start.1 = (f32[1536,256]{1,0:T(8,128)S(1)}, f32[1536,256]{1,0:T(8,128)}, u32[]{:S(2)}, u32[]{:S(2)}) collective-permute-start(f32[1536,256]{1,0:T(8,128)S(1)} %broadcast_select_fusion.6), channel_id=1, source_target_pairs={{0,8},{4,12},{8,0},{12,4},{1,9},{5,13},{9,1},{13,5},{2,10},{6,14},... | collective-permute-start | bytes 4718600 | tf_op jit(solution)/shard_map/ppermute | solution.py:29
  180.4 157.1 %all-reduce.7.cloned.1.call-start = ((), (), s32[]{:S(2)}) async-start(), calls=%async_computation.3 | async-start | bytes 3145728 | tf_op jit(solution)/shard_map/psum | solution.py:18
  257.9 3.8 collective-permute-start.2
  261.5 4.5 copy-start.3
  264.5 37.0 %collective-permute-start.3 = (f32[1536,256]{1,0:T(8,128)}, f32[1536,256]{1,0:T(8,128)}, u32[]{:S(2)}, u32[]{:S(2)}) collective-permute-start(f32[1536,256]{1,0:T(8,128)} %broadcast_select_fusion.4), channel_id=1, source_target_pairs={{0,8},{4,12},{8,0},{12,4},{1,9},{5,13},{9,1},{13,5},{2,10},{6,14},... | collective-permute-start | bytes 4718600 | tf_op jit(solution)/shard_map/ppermute | solution.py:29
  270.1 153.4 %all-reduce.9.cloned.1.call-start = ((), (), s32[]{:S(2)}) async-start(), calls=%async_computation.4 | async-start | bytes 3145728 | tf_op jit(solution)/shard_map/psum | solution.py:18
  344.0 3.8 collective-permute-start.4
  346.2 5.8 %copy-start.4 = (f32[256,1536]{1,0:T(8,128)S(1)}, f32[256,1536]{1,0:T(8,128)}, u32[]{:S(2)}) copy-start(f32[256,1536]{1,0:T(8,128)} %all-reduce.7.cloned.1.call-done) | copy-start | bytes 4718596
  350.5 36.8 %collective-permute-start.5 = (f32[1536,256]{1,0:T(8,128)}, f32[1536,256]{1,0:T(8,128)}, u32[]{:S(2)}, u32[]{:S(2)}) collective-permute-start(f32[1536,256]{1,0:T(8,128)} %broadcast_select_fusion.2), channel_id=1, source_target_pairs={{0,8},{4,12},{8,0},{12,4},{1,9},{5,13},{9,1},{13,5},{2,10},{6,14},... | collective-permute-start | bytes 4718600 | tf_op jit(solution)/shard_map/ppermute | solution.py:29
  356.1 147.9 %all-reduce.11.cloned.1.call-start = ((), (), s32[]{:S(2)}) async-start(), calls=%async_computation.5 | async-start | bytes 3145728 | tf_op jit(solution)/shard_map/psum | solution.py:18
  426.5 4.9 copy-start.5
  430.1 5.4 %collective-permute-start.6 = (f32[1536,256]{1,0:T(8,128)}, f32[1536,256]{1,0:T(8,128)}, u32[]{:S(2)}, u32[]{:S(2)}) collective-permute-start(f32[1536,256]{1,0:T(8,128)} %fusion.11), channel_id=1, source_target_pairs={{0,4},{4,0},{8,12},{12,8},{1,5},{5,1},{9,13},{13,9},{2,6},{6,2},{1... | collective-permute-start | bytes 4718600 | tf_op jit(solution)/shard_map/ppermute | solution.py:29
  437.2 66.8 %collective-permute-start.7 = (f32[1536,256]{1,0:T(8,128)S(1)}, f32[1536,256]{1,0:T(8,128)}, u32[]{:S(2)}, u32[]{:S(2)}) collective-permute-start(f32[1536,256]{1,0:T(8,128)S(1)} %broadcast_select_fusion), channel_id=1, source_target_pairs={{0,8},{4,12},{8,0},{12,4},{1,9},{5,13},{9,1},{13,5},{2,10},{6,14},... | collective-permute-start | bytes 4718600 | tf_op jit(solution)/shard_map/ppermute | solution.py:29
  520.3 2.9 copy-start.1
Sparse Core Ops, SparseCore 0:
  180.6 70.8 all-reduce.4
  270.3 67.2 all-reduce.6
  356.2 67.2 all-reduce.8
  435.7 68.3 all-reduce.10

commit v5 on v4

--- a/solution.py
+++ b/solution.py
@@ -162,6 +162,15 @@
             col_owner, row_owner, col_offset, row_offset = strip_bounds(step_index + 1)
             top_part = lax.dynamic_slice_in_dim(top_strip, col_offset, PANEL, 1)
             left_part = lax.dynamic_slice_in_dim(left_strip, row_offset, PANEL, 0)
+            next_row = jnp.where(
+                active_cols[None, :],
+                next_row
+                - jnp.dot(
+                    left_part, top_strip, precision=HIGHEST, preferred_element_type=jnp.float32
+                ),
+                next_row,
+            )
+            next_row, next_col = lax.optimization_barrier((next_row, next_col))
             next_col = jnp.where(
                 active_rows[:, None],
                 next_col
@@ -169,14 +178,6 @@
                     left_strip, top_part, precision=HIGHEST, preferred_element_type=jnp.float32
                 ),
                 next_col,
-            )
-            next_row = jnp.where(
-                active_cols[None, :],
-                next_row
-                - jnp.dot(
-                    left_part, top_strip, precision=HIGHEST, preferred_element_type=jnp.float32
-                ),
-                next_row,
             )
             left_next, top_next = share_strips(next_col, next_row, step_index + 1)
         eliminate_matrix = matrix

time: 535 us -> 529 us (0.989)
  local copies, waits for them, and re-layouts: 47 us -> 58.7 us
  waiting for transfers between devices: 304 us -> 297 us
    psum x4, waiting for transfers between devices: 155 us -> 145 us  [broadcast(): return lax.psum(block, axis)]
    unnamed x16 -> x24, local copies, waits for them, and re-layouts: 16.8 us -> 24.3 us
    select_n x1 -> x4, other arithmetic: 2.65 us -> 9.29 us  [broadcast(): jnp.where(lax.axis_index(axis) == source, block, jnp.zeros_like(block))]
    select_n x7, other arithmetic: 12.4 us -> 5.87 us  [exchange_broadcast(): block = jnp.where(take, received, block)]
  transfers between devices with their start and end apart: 14 -> 14, of which waited for: 11 -> 10; matrix products, arithmetic and copies ran while one was open for 17% -> 15% of each run, Pallas kernels for 0% -> 0%
where the time goes in v5:
time: 529 us; the launch traced here: 525 us
  waiting for transfers between devices  297 us (56%)
  matrix products  81.4 us (15%)
  local copies, waits for them, and re-layouts  58.7 us (11%)
  other arithmetic  44.8 us (8%)
  between operations  22 us (4%)
  starting transfers between devices  21.3 us (4%)
    psum x4, waiting for transfers between devices, broadcast(): return lax.psum(block, axis)  145 us
    all_to_all x1, waiting for transfers between devices, body(): lax.all_to_all(payload, ('front', 'column', 'row'), split_axis=0, concat_...  84.1 us
    ppermute x8, waiting for transfers between devices, exchange_broadcast(): received = lax.ppermute(block, axis, partner)  67.3 us
    dot_general x4, matrix products, body(): jnp.dot(left_strip, top_strip, precision=HIGHEST, preferred_element_type=...  49.9 us
    unnamed x24, local copies, waits for them, and re-layouts  24.3 us
    scatter-add x1, local copies, waits for them, and re-layouts, scatter_tiles(): grid.at[tile_rows, :, tile_cols, :]  14.5 us
    dot_general x3, matrix products, body(): jnp.dot(left_part, top_strip, precision=HIGHEST, preferred_element_type=j...  13.9 us
    scatter-add x1, other arithmetic, scatter_tiles(): grid.at[tile_rows, :, tile_cols, :]  13.8 us
  transfers between devices with their start and end apart: 14, of which 10 were waited for; matrix products, arithmetic and copies ran while one was open for 15% of the time, Pallas kernels for 0%

profile of v5, /device:TPU:0, one launch (start us, length us, event | category | flops | bytes accessed | tf_op | source)
XLA Modules:
  0.0 525.1 jit_solution(5768119713932160908)
XLA Ops:
  10.7 7.3 %all-to-all-start = ((s32[32,1,2]{2,1,0:T(1,128)}), s32[32,1,2]{2,1,0:T(1,128)S(1)}, u32[]{:S(2)}, u32[]{:S(2)}) async-start(s32[32,1,2]{2,1,0:T(1,128)} %bitcast.9), calls=%async_computation | async-start | bytes 32768 | tf_op jit(solution)/shard_map/all_to_all | solution.py:111
  18.0 2.9 reshape_squeeze.3
  20.9 1.9 copy.16
  22.8 2.5 broadcast_in_dim.159
  25.3 5.4 %scatter_fusion = f32[64,128,128]{2,1,0:T(8,128)} fusion(f32[64,128,128]{2,1,0:T(8,128)} %broadcast_in_dim.159, s32[32]{0:T(128)S(1)} %fusion.46, f32[32,128,128]{2,1,0:T(8,128)S(1)} %bitcast.94), kind=kCustom, calls=%fused_computation.1 | custom fusion | bytes 6291584 | tf_op jit(solution)/shard_map/scatter | solution.py:44
  30.7 5.9 %all-to-all-start.1 = ((f32[32,2,128,128]{3,2,1,0:T(8,128)}), f32[32,2,128,128]{3,2,1,0:T(8,128)}, u32[]{:S(2)}, u32[]{:S(2)}) async-start(f32[32,2,128,128]{3,2,1,0:T(8,128)} %bitcast.93), calls=%async_computation.1 | async-start | bytes 8388608 | tf_op jit(solution)/shard_map/all_to_all | solution.py:108
  38.1 4.4 compare_select_fusion
  43.1 84.1 %all-to-all-done.1 = f32[32,2,128,128]{3,2,1,0:T(8,128)} async-done(((f32[32,2,128,128]{3,2,1,0:T(8,128)}), f32[32,2,128,128]{3,2,1,0:T(8,128)}, u32[]{:S(2)}, u32[]{:S(2)}) %all-to-all-start.1) | async-done | bytes 4194336 | tf_op jit(solution)/shard_map/all_to_all | solution.py:108
  127.2 13.8 %scatter_fusion.1 = f32[12,128,12,128]{3,1,2,0:T(8,128)} fusion(f32[12,128,12,128]{3,1,2,0:T(8,128)} %compare_select_fusion, s32[64]{0:T(128)S(1)} %fusion.45, f32[64,128,128]{2,1,0:T(8,128)} %bitcast.14), kind=kCustom, calls=%fused_computation.2 | custom fusion | flops 1048576 | bytes 12583424 | tf_op jit(solution)/shard_map/scatter-add | solution.py:62
  141.0 14.5 %copy.17 = f32[12,128,12,128]{3,2,1,0:T(8,128)} copy(f32[12,128,12,128]{3,1,2,0:T(8,128)} %scatter_fusion.1) | data formatting | bytes 18874368 | tf_op jit(solution)/shard_map/scatter-add | solution.py:62
  155.5 9.3 %copy.20 = f32[192,8,12,128]{3,1,2,0:T(8,128)S(1)} copy(f32[192,8,12,128]{3,2,1,0:T(8,128)} %bitcast.91) | data formatting | bytes 18874368
  164.8 3.7 copy-done.2
  168.5 2.9 fusion.6
  171.4 1.7 collective-permute-start
  174.5 1.9 collective-permute-done
  178.1 2.6 dynamic-slice_select_fusion
  182.9 2.7 constant_dynamic-slice_fusion.2
  185.6 27.7 %collective-permute-done.1 = f32[1536,256]{1,0:T(8,128)} collective-permute-done((f32[1536,256]{1,0:T(8,128)S(1)}, f32[1536,256]{1,0:T(8,128)}, u32[]{:S(2)}, u32[]{:S(2)}) %collective-permute-start.1) | collective-permute-done | bytes 1572896 | tf_op jit(solution)/shard_map/ppermute | solution.py:29
  213.6 37.8 %all-reduce.5.cloned.1.call-done = f32[256,1536]{1,0:T(8,128)} async-done(((f32[256,1536]{1,0:T(8,128)}), f32[256,1536]{1,0:T(8,128)}) %all-reduce.5.cloned.1.call-update) | async-done | bytes 1572880 | tf_op jit(solution)/shard_map/psum | solution.py:18
  251.5 4.7 fusion.5
  257.6 3.5 fusion.12
  264.1 2.7 broadcast_select_fusion.2
  266.8 1.6 broadcast_select_fusion.7
  268.4 1.6 collective-permute-start.3
  270.0 12.0 %subtract_select_fusion.3 = f32[1536,1536]{1,0:T(8,128)S(1)} fusion(f32[1536,1536]{1,0:T(8,128)} %bitcast.90, f32[1536,256]{1,0:T(8,128)S(1)} %broadcast_select_fusion.10, f32[256,1536]{1,0:T(8,128)S(1)} %copy-done.5, pred[1536]{0:T(1024)(128)(4,1)S(1)} %broadcast_compare_fusion, pred[1536]{0:T(1024)(128)(4,1)S(1)} %broadcast_compare_fusion.1), kind=kOutput, calls=%fused_computation.6 | convolution fusion | flops 7254835200 | bytes 22023168 | tf_op jit(solution)/shard_map/dot_general | solution.py:185
  282.5 3.7 copy-done.3
  287.5 17.7 %collective-permute-done.3 = f32[1536,256]{1,0:T(8,128)S(1)} collective-permute-done((f32[1536,256]{1,0:T(8,128)S(1)}, f32[1536,256]{1,0:T(8,128)S(1)}, u32[]{:S(2)}, u32[]{:S(2)}) %collective-permute-start.3) | collective-permute-done | bytes 1572896 | tf_op jit(solution)/shard_map/ppermute | solution.py:29
  305.5 29.7 %all-reduce.7.cloned.1.call-done = f32[256,1536]{1,0:T(8,128)} async-done(((f32[256,1536]{1,0:T(8,128)}), f32[256,1536]{1,0:T(8,128)}) %all-reduce.7.cloned.1.call-update) | async-done | bytes 1572880 | tf_op jit(solution)/shard_map/psum | solution.py:18
  335.2 4.7 fusion.3
  341.4 3.5 fusion.10
  347.1 2.7 broadcast_select_fusion.1
  349.9 1.6 broadcast_select_fusion.5
  351.5 1.5 collective-permute-start.5
  353.0 11.9 %subtract_select_fusion.2 = f32[1536,1536]{1,0:T(8,128)S(1)} fusion(f32[1536,1536]{1,0:T(8,128)} %copy-done.3, f32[1536,256]{1,0:T(8,128)S(1)} %broadcast_select_fusion.8, f32[256,1536]{1,0:T(8,128)S(1)} %copy-done.6, pred[1536]{0:T(1024)(128)(4,1)S(1)} %get-tuple-element.24, pred[1536]{0:T(1024)(128)(4,1)S(1)} %get-tuple-element.23), kind=kOutput, calls=%fused_computation.5 | convolution fusion | flops 7254835200 | bytes 22023168 | tf_op jit(solution)/shard_map/dot_general | solution.py:185
  365.4 3.7 copy-done.4
  369.3 19.0 %collective-permute-done.5 = f32[1536,256]{1,0:T(8,128)S(1)} collective-permute-done((f32[1536,256]{1,0:T(8,128)S(1)}, f32[1536,256]{1,0:T(8,128)S(1)}, u32[]{:S(2)}, u32[]{:S(2)}) %collective-permute-start.5) | collective-permute-done | bytes 1572896 | tf_op jit(solution)/shard_map/ppermute | solution.py:29
  388.6 28.9 %all-reduce.9.cloned.1.call-done = f32[256,1536]{1,0:T(8,128)} async-done(((f32[256,1536]{1,0:T(8,128)}), f32[256,1536]{1,0:T(8,128)}) %all-reduce.9.cloned.1.call-update) | async-done | bytes 1572880 | tf_op jit(solution)/shard_map/psum | solution.py:18
  417.5 4.6 fusion.1
  422.0 2.4 fusion
  424.4 2.4 fusion.8
  430.4 1.6 broadcast_select_fusion.3
  432.0 1.5 collective-permute-start.7
  433.8 13.7 %subtract_select_fusion.1 = f32[1536,1536]{1,0:T(8,128)} fusion(f32[1536,1536]{1,0:T(8,128)} %copy-done.4, f32[1536,256]{1,0:T(8,128)S(1)} %broadcast_select_fusion.6, f32[256,1536]{1,0:T(8,128)} %all-reduce.9.cloned.1.call-done, pred[1536]{0:T(1024)(128)(4,1)S(1)} %get-tuple-element.22, pred[1536]{0:T(1024)(128)(4,1)S(1)} %get-tuple-element.21), kind=kOutput, calls=%fused_computation.4 | convolution fusion | flops 7254835200 | bytes 22023168 | tf_op jit(solution)/shard_map/dot_general | solution.py:185
  447.5 2.9 select_dynamic-update-slice_fusion
  450.4 48.9 %all-reduce.11.cloned.1.call-done = f32[256,1536]{1,0:T(8,128)} async-done(((f32[256,1536]{1,0:T(8,128)}), f32[256,1536]{1,0:T(8,128)}) %all-reduce.11.cloned.1.call-update) | async-done | bytes 1572880 | tf_op jit(solution)/shard_map/psum | solution.py:18
  499.3 12.3 %subtract_select_fusion = f32[1536,1536]{1,0:T(8,128)S(1)} fusion(f32[1536,1536]{1,0:T(8,128)} %select_dynamic-update-slice_fusion, f32[256,1536]{1,0:T(8,128)} %all-reduce.11.cloned.1.call-done, pred[1536]{0:T(1024)(128)(4,1)S(1)} %get-tuple-element.20, pred[1536]{0:T(1024)(128)(4,1)S(1)} %get-tuple-element.19, f32[1536,256]{1,0:T(8,128)} %collective-permute-done.7, ...), kind=kOutput, calls=%fused_computation.3 | convolution fusion | flops 7255228416 | bytes 23596032 | tf_op jit(solution)/shard_map/dot_general | solution.py:185
  511.7 3.7 copy.30
  515.4 2.9 bitcast_dynamic-update-slice_fusion
  (92 shorter events, 18.1 us)
Async XLA Ops:
  6.5 31.5 %copy-start = (f32[1,6144]{1,0:T(1,128)S(1)}, f32[1,6144]{1,0:T(1,128)}, u32[]{:S(2)}) copy-start(f32[1,6144]{1,0:T(1,128)} %param.11) | copy-start | bytes 73732
  10.7 20.0 %all-to-all-start = ((s32[32,1,2]{2,1,0:T(1,128)}), s32[32,1,2]{2,1,0:T(1,128)S(1)}, u32[]{:S(2)}, u32[]{:S(2)}) async-start(s32[32,1,2]{2,1,0:T(1,128)} %bitcast.9), calls=%async_computation | async-start | bytes 32768 | tf_op jit(solution)/shard_map/all_to_all | solution.py:111
  30.7 6.0 %copy-start.10 = (s32[1,4]{1,0:T(1,128)S(1)}, s32[1,4]{1,0:T(1,128)}, u32[]{:S(2)}) copy-start(s32[1,4]{1,0:T(1,128)} %param.12) | copy-start | bytes 52
  30.7 96.5 %all-to-all-start.1 = ((f32[32,2,128,128]{3,2,1,0:T(8,128)}), f32[32,2,128,128]{3,2,1,0:T(8,128)}, u32[]{:S(2)}, u32[]{:S(2)}) async-start(f32[32,2,128,128]{3,2,1,0:T(8,128)} %bitcast.93), calls=%async_computation.1 | async-start | bytes 8388608 | tf_op jit(solution)/shard_map/all_to_all | solution.py:108
  36.7 214.8 %all-reduce.5.cloned.1.call-start = ((), (), s32[]{:S(2)}) async-start(), calls=%async_computation.2 | async-start | bytes 3145728 | tf_op jit(solution)/shard_map/psum | solution.py:18
  164.7 3.7 copy-start.2
  171.4 4.9 collective-permute-start
  176.7 36.7 %collective-permute-start.1 = (f32[1536,256]{1,0:T(8,128)S(1)}, f32[1536,256]{1,0:T(8,128)}, u32[]{:S(2)}, u32[]{:S(2)}) collective-permute-start(f32[1536,256]{1,0:T(8,128)S(1)} %broadcast_select_fusion.9), channel_id=1, source_target_pairs={{0,8},{4,12},{8,0},{12,4},{1,9},{5,13},{9,1},{13,5},{2,10},{6,14},... | collective-permute-start | bytes 4718600 | tf_op jit(solution)/shard_map/ppermute | solution.py:29
  180.8 154.4 %all-reduce.7.cloned.1.call-start = ((), (), s32[]{:S(2)}) async-start(), calls=%async_computation.3 | async-start | bytes 3145728 | tf_op jit(solution)/shard_map/psum | solution.py:18
  251.5 4.7 copy-start.5
  251.5 4.7 copy-start.9
  261.1 5.7 %collective-permute-start.2 = (f32[1536,256]{1,0:T(8,128)}, f32[1536,256]{1,0:T(8,128)}, u32[]{:S(2)}, u32[]{:S(2)}) collective-permute-start(f32[1536,256]{1,0:T(8,128)} %fusion.12), channel_id=1, source_target_pairs={{0,4},{4,0},{8,12},{12,8},{1,5},{5,1},{9,13},{13,9},{2,6},{6,2},{1... | collective-permute-start | bytes 4718600 | tf_op jit(solution)/shard_map/ppermute | solution.py:29
  266.7 150.7 %all-reduce.9.cloned.1.call-start = ((), (), s32[]{:S(2)}) async-start(), calls=%async_computation.4 | async-start | bytes 3145728 | tf_op jit(solution)/shard_map/psum | solution.py:18
  268.4 36.9 %collective-permute-start.3 = (f32[1536,256]{1,0:T(8,128)S(1)}, f32[1536,256]{1,0:T(8,128)S(1)}, u32[]{:S(2)}, u32[]{:S(2)}) collective-permute-start(f32[1536,256]{1,0:T(8,128)S(1)} %broadcast_select_fusion.7), channel_id=1, source_target_pairs={{0,8},{4,12},{8,0},{12,4},{1,9},{5,13},{9,1},{13,5},{2,10},{6,14},... | collective-permute-start | bytes 4718600 | tf_op jit(solution)/shard_map/ppermute | solution.py:29
  282.5 3.7 copy-start.3
  335.2 4.7 copy-start.6
  335.2 4.7 copy-start.8
  344.9 5.0 collective-permute-start.4
  349.8 149.5 %all-reduce.11.cloned.1.call-start = ((), (), s32[]{:S(2)}) async-start(), calls=%async_computation.5 | async-start | bytes 3145728 | tf_op jit(solution)/shard_map/psum | solution.py:18
  351.5 36.9 %collective-permute-start.5 = (f32[1536,256]{1,0:T(8,128)S(1)}, f32[1536,256]{1,0:T(8,128)S(1)}, u32[]{:S(2)}, u32[]{:S(2)}) collective-permute-start(f32[1536,256]{1,0:T(8,128)S(1)} %broadcast_select_fusion.5), channel_id=1, source_target_pairs={{0,8},{4,12},{8,0},{12,4},{1,9},{5,13},{9,1},{13,5},{2,10},{6,14},... | collective-permute-start | bytes 4718600 | tf_op jit(solution)/shard_map/ppermute | solution.py:29
  365.4 3.7 copy-start.4
  426.8 2.7 copy-start.7
  426.8 3.6 collective-permute-start.6
  432.0 67.3 %collective-permute-start.7 = (f32[1536,256]{1,0:T(8,128)S(1)}, f32[1536,256]{1,0:T(8,128)}, u32[]{:S(2)}, u32[]{:S(2)}) collective-permute-start(f32[1536,256]{1,0:T(8,128)S(1)} %broadcast_select_fusion.3), channel_id=1, source_target_pairs={{0,8},{4,12},{8,0},{12,4},{1,9},{5,13},{9,1},{13,5},{2,10},{6,14},... | collective-permute-start | bytes 4718600 | tf_op jit(solution)/shard_map/ppermute | solution.py:29
  515.4 2.9 copy-start.1
Sparse Core Ops, SparseCore 0:
  180.9 70.5 all-reduce.4
  266.9 68.3 all-reduce.6
  349.9 67.4 all-reduce.8
  429.6 69.6 all-reduce.10

commit v6 on v5

--- a/solution.py
+++ b/solution.py
@@ -63,6 +63,57 @@
         payload.reshape(-1, tile_side, tile_side), mode="drop"
     )
     return grid.reshape(row_tiles * tile_side, col_tiles * tile_side)
+
+
+def arrival_labels(
+    row_map, col_map, child_size, groups, row_devs, col_devs, piece_rows, piece_cols,
+    row_tiles, col_tiles, sentinel,
+):
+    children, side = row_map.shape[1], row_map.shape[2]
+    span = children * side
+    maps = jnp.concatenate(
+        [row_map[0].reshape(-1), col_map[0].reshape(-1), child_size[0].reshape(-1)]
+    )
+    every = lax.all_gather(maps, "front")
+    front_id = lax.axis_index("front")
+    row_maps = every[:, :span].reshape(groups, children, side)[:, front_id]
+    col_maps = every[:, span : 2 * span].reshape(groups, children, side)[:, front_id]
+    sizes = every[:, 2 * span :].reshape(groups, children)[:, front_id]
+    child_rows = (
+        jnp.arange(row_devs, dtype=jnp.int32)[:, None] * piece_rows
+        + jnp.arange(piece_rows, dtype=jnp.int32)[None, :]
+    )
+    child_cols = (
+        jnp.arange(col_devs, dtype=jnp.int32)[:, None] * piece_cols
+        + jnp.arange(piece_cols, dtype=jnp.int32)[None, :]
+    )
+    parent_rows = row_maps[:, child_rows]
+    parent_cols = col_maps[:, child_cols]
+    hit_rows = (child_rows[None] < sizes[:, None, None]) & (
+        parent_rows // row_tiles == lax.axis_index("row")
+    )
+    hit_cols = (child_cols[None] < sizes[:, None, None]) & (
+        parent_cols // col_tiles == lax.axis_index("column")
+    )
+    hit = hit_cols[:, :, None, None, :] & hit_rows[:, None, :, :, None]
+    spot = (parent_rows % row_tiles)[:, None, :, :, None] * col_tiles + (
+        parent_cols % col_tiles
+    )[:, :, None, None, :]
+    sources = groups * col_devs * row_devs
+    hit = hit.reshape(sources, piece_rows * piece_cols).astype(jnp.int32)
+    spot = jnp.broadcast_to(
+        spot, (groups, col_devs, row_devs, piece_rows, piece_cols)
+    ).reshape(sources, piece_rows * piece_cols)
+    rank = jnp.cumsum(hit, axis=1) - hit
+    slots = []
+    for slot in range(ROWMOST):
+        chosen = (hit == 1) & (rank == slot)
+        slots.append(
+            jnp.where(
+                jnp.any(chosen, axis=1), jnp.sum(jnp.where(chosen, spot, 0), axis=1), sentinel
+            )
+        )
+    return jnp.stack(slots, axis=1)
 
 
 def body(cbs, row_map, col_map, child_size, front_diag, panel_order, pivot_inverse):
@@ -104,11 +155,12 @@
     payload, labels = pack_tiles(
         tile_stack, whole_target, target_spot, all_devices, ROWMOST, sentinel
     )
-    arrived, arrived_labels = (
-        lax.all_to_all(
-            payload, ("front", "column", "row"), split_axis=0, concat_axis=0, tiled=True
-        ),
-        lax.all_to_all(labels, ("front", "column", "row"), split_axis=0, concat_axis=0, tiled=True),
+    arrived = lax.all_to_all(
+        payload, ("front", "column", "row"), split_axis=0, concat_axis=0, tiled=True
+    )
+    arrived_labels = arrival_labels(
+        row_map, col_map, child_size, groups, row_devs, col_devs, piece_rows, piece_cols,
+        row_tiles, col_tiles, sentinel,
     )
     row_glob = row_id * local_rows + jnp.arange(local_rows, dtype=jnp.int32)
     col_glob = col_id * local_cols + jnp.arange(local_cols, dtype=jnp.int32)
@@ -150,11 +202,15 @@
             col_strip, inverses[step_index], precision=HIGHEST, preferred_element_type=jnp.float32
         )
         left_strip = exchange_broadcast(owner_left, "column", col_owner)
-        top_strip = broadcast(row_strip, "row", row_owner)
+        top_strip = lax.psum(row_strip, "row")
         return (left_strip, top_strip)
 
+    def owned_rows(row_strip, step_index):
+        col_owner, row_owner, col_offset, row_offset = strip_bounds(step_index)
+        return jnp.where(row_id == row_owner, row_strip, jnp.zeros_like(row_strip))
+
     first_col, first_row = current_strips(matrix, 0)
-    left_strip, top_strip = share_strips(first_col, first_row, 0)
+    left_strip, top_strip = share_strips(first_col, owned_rows(first_row, 0), 0)
     for step_index in range(PANELS):
         if step_index + 1 < PANELS:
             active_rows, active_cols = actives(step_index)
@@ -170,6 +226,7 @@
                 ),
                 next_row,
             )
+            next_row = owned_rows(next_row, step_index + 1)
             next_row, next_col = lax.optimization_barrier((next_row, next_col))
             next_col = jnp.where(
                 active_rows[:, None],

time: 529 us -> 515 us (0.974)
  waiting for transfers between devices: 297 us -> 270 us
  blocking collectives: 0 us -> 17.3 us
  other arithmetic: 44.8 us -> 38.6 us
  starting transfers between devices: 21.3 us -> 15.5 us
    all_to_all x1, waiting for transfers between devices: 84.1 us -> 60.5 us  [body(): lax.all_to_all(payload, ('front', 'column', 'row'), split_axis=0, concat_...]
    unnamed x0 -> x1, blocking collectives: none -> 17.3 us
    all_to_all x1 -> x0, starting transfers between devices: 7.3 us -> none  [body(): lax.all_to_all(labels, ('front', 'column', 'row'), split_axis=0, concat_a...]
    psum x4, waiting for transfers between devices: 145 us -> 140 us  [share_strips(): top_strip = lax.psum(row_strip, 'row')]
    select_n x6 -> x7, other arithmetic: 9.32 us -> 3.54 us  [the longest x1 2.65 us: owned_rows(): return jnp.where(row_id == row_owner, row_strip, jnp.zeros_like(row_strip))]
    unnamed x24 -> x30, local copies, waits for them, and re-layouts: 24.3 us -> 25.8 us
  transfers between devices with their start and end apart: 14 -> 13, of which waited for: 10 -> 12; matrix products, arithmetic and copies ran while one was open for 15% -> 13% of each run, Pallas kernels for 0% -> 0%
where the time goes in v6:
time: 515 us; the launch traced here: 510 us
  waiting for transfers between devices  270 us (52%)
  matrix products  83.1 us (16%)
  local copies, waits for them, and re-layouts  62.7 us (12%)
  other arithmetic  38.6 us (7%)
  between operations  22.6 us (4%)
  blocking collectives  17.3 us (3%)
  starting transfers between devices  15.5 us (3%)
    psum x4, waiting for transfers between devices, share_strips(): top_strip = lax.psum(row_strip, 'row')  140 us
    ppermute x8, waiting for transfers between devices, exchange_broadcast(): received = lax.ppermute(block, axis, partner)  69.7 us
    all_to_all x1, waiting for transfers between devices, body(): lax.all_to_all(payload, ('front', 'column', 'row'), split_axis=0, concat_...  60.5 us
    dot_general x4, matrix products, body(): jnp.dot(left_strip, top_strip, precision=HIGHEST, preferred_element_type=...  49 us
    unnamed x30, local copies, waits for them, and re-layouts  25.8 us
    unnamed x1, blocking collectives  17.3 us
    scatter-add x1, local copies, waits for them, and re-layouts, scatter_tiles(): grid.at[tile_rows, :, tile_cols, :]  14.5 us
    dot_general x3, matrix products, body(): jnp.dot(left_part, top_strip, precision=HIGHEST, preferred_element_type=j...  14 us
  transfers between devices with their start and end apart: 13, of which 12 were waited for; matrix products, arithmetic and copies ran while one was open for 13% of the time, Pallas kernels for 0%

profile of v6, /device:TPU:0, one launch (start us, length us, event | category | flops | bytes accessed | tf_op | source)
XLA Modules:
  0.0 509.7 jit_solution(3860339028783931139)
XLA Ops:
  9.1 2.9 reshape_squeeze.11
  12.0 1.9 copy.105
  13.9 2.5 broadcast_in_dim.96
  16.4 5.4 %scatter_fusion = f32[64,128,128]{2,1,0:T(8,128)} fusion(f32[64,128,128]{2,1,0:T(8,128)} %broadcast_in_dim.96, s32[32]{0:T(128)S(1)} %fusion.54, f32[32,128,128]{2,1,0:T(8,128)S(1)} %bitcast.159), kind=kCustom, calls=%fused_computation.2 | custom fusion | bytes 6291584 | tf_op jit(solution)/shard_map/scatter | solution.py:44
  21.9 7.4 %all-to-all-start = ((f32[32,2,128,128]{3,2,1,0:T(8,128)}), f32[32,2,128,128]{3,2,1,0:T(8,128)}, u32[]{:S(2)}, u32[]{:S(2)}) async-start(f32[32,2,128,128]{3,2,1,0:T(8,128)} %bitcast.158), calls=%async_computation | async-start | bytes 8388608 | tf_op jit(solution)/shard_map/all_to_all | solution.py:158
  32.3 17.3 %all-reduce = s32[132]{0:T(256)S(1)} all-reduce(s32[132]{0:T(256)S(1)} %add_dynamic-update-slice_fusion), channel_id=2, replica_groups=mesh['front'=2,'column'=4,'row'=4] {'front'}, use_global_device_ids=true, to_apply=%add | all-reduce | flops 132 | bytes 1056
  54.8 4.4 compare_select_fusion
  59.2 60.5 %all-to-all-done = f32[32,2,128,128]{3,2,1,0:T(8,128)} async-done(((f32[32,2,128,128]{3,2,1,0:T(8,128)}), f32[32,2,128,128]{3,2,1,0:T(8,128)}, u32[]{:S(2)}, u32[]{:S(2)}) %all-to-all-start) | async-done | bytes 4194336 | tf_op jit(solution)/shard_map/all_to_all | solution.py:158
  119.8 13.8 %scatter_fusion.1 = f32[12,128,12,128]{3,1,2,0:T(8,128)} fusion(f32[12,128,12,128]{3,1,2,0:T(8,128)} %compare_select_fusion, s32[64]{0:T(128)S(1)} %fusion.53, f32[64,128,128]{2,1,0:T(8,128)} %bitcast.26), kind=kCustom, calls=%fused_computation.3 | custom fusion | flops 1048576 | bytes 12583424 | tf_op jit(solution)/shard_map/scatter-add | solution.py:62
  133.6 14.5 %copy.106 = f32[12,128,12,128]{3,2,1,0:T(8,128)} copy(f32[12,128,12,128]{3,1,2,0:T(8,128)} %scatter_fusion.1) | data formatting | bytes 18874368 | tf_op jit(solution)/shard_map/scatter-add | solution.py:62
  148.1 9.3 %copy.109 = f32[192,8,12,128]{3,1,2,0:T(8,128)S(1)} copy(f32[192,8,12,128]{3,2,1,0:T(8,128)} %bitcast.156) | data formatting | bytes 18874368
  157.4 3.7 copy-done.2
  161.1 2.7 fusion.9
  163.8 1.7 collective-permute-start
  166.9 1.8 collective-permute-done
  168.9 1.6 collective-permute-start.1
  170.6 2.6 dynamic-slice_select_fusion
  176.2 2.7 constant_dynamic-slice_fusion.2
  178.8 26.8 %collective-permute-done.1 = f32[1536,256]{1,0:T(8,128)} collective-permute-done((f32[1536,256]{1,0:T(8,128)S(1)}, f32[1536,256]{1,0:T(8,128)}, u32[]{:S(2)}, u32[]{:S(2)}) %collective-permute-start.1) | collective-permute-done | bytes 1572896 | tf_op jit(solution)/shard_map/ppermute | solution.py:29
  205.6 1.7 broadcast_select_fusion.7
  207.3 36.5 %all-reduce.6.cloned.1.call-done = f32[256,1536]{1,0:T(8,128)} async-done(((f32[256,1536]{1,0:T(8,128)}), f32[256,1536]{1,0:T(8,128)}) %all-reduce.6.cloned.1.call-update) | async-done | bytes 1572880 | tf_op jit(solution)/shard_map/psum | solution.py:205
  243.9 4.7 fusion.8
  248.6 2.9 fusion.6
  251.4 3.5 fusion.15
  258.7 1.6 broadcast_select_fusion.4
  261.8 12.0 %subtract_select_fusion.3 = f32[1536,1536]{1,0:T(8,128)S(1)} fusion(f32[1536,1536]{1,0:T(8,128)} %bitcast.155, f32[1536,256]{1,0:T(8,128)S(1)} %broadcast_select_fusion.7, f32[256,1536]{1,0:T(8,128)S(1)} %copy-done.5, pred[1536]{0:T(1024)(128)(4,1)S(1)} %get-tuple-element.48, pred[1536]{0:T(1024)(128)(4,1)S(1)} %get-tuple-element.49), kind=kOutput, calls=%fused_computation.7 | convolution fusion | flops 7254835200 | bytes 22023168 | tf_op jit(solution)/shard_map/dot_general | solution.py:242
  274.4 3.7 copy-done.3
  279.4 17.4 %collective-permute-done.3 = f32[1536,256]{1,0:T(8,128)S(1)} collective-permute-done((f32[1536,256]{1,0:T(8,128)S(1)}, f32[1536,256]{1,0:T(8,128)S(1)}, u32[]{:S(2)}, u32[]{:S(2)}) %collective-permute-start.3) | collective-permute-done | bytes 1572896 | tf_op jit(solution)/shard_map/ppermute | solution.py:29
  297.0 29.2 %all-reduce.8.cloned.1.call-done = f32[256,1536]{1,0:T(8,128)} async-done(((f32[256,1536]{1,0:T(8,128)}), f32[256,1536]{1,0:T(8,128)}) %all-reduce.8.cloned.1.call-update) | async-done | bytes 1572880 | tf_op jit(solution)/shard_map/psum | solution.py:205
  326.2 4.7 fusion.5
  330.9 2.9 fusion.3
  333.8 3.5 fusion.13
  339.4 1.7 collective-permute-done.4
  341.0 1.6 broadcast_select_fusion.2
  344.2 11.7 %subtract_select_fusion.2 = f32[1536,1536]{1,0:T(8,128)S(1)} fusion(f32[1536,1536]{1,0:T(8,128)} %copy-done.3, f32[1536,256]{1,0:T(8,128)S(1)} %broadcast_select_fusion.5, f32[256,1536]{1,0:T(8,128)S(1)} %copy-done.6, pred[1536]{0:T(1024)(128)(4,1)S(1)} %get-tuple-element.24, pred[1536]{0:T(1024)(128)(4,1)S(1)} %get-tuple-element.23), kind=kOutput, calls=%fused_computation.6 | convolution fusion | flops 7254835200 | bytes 22023168 | tf_op jit(solution)/shard_map/dot_general | solution.py:242
  356.4 3.7 copy-done.4
  360.3 18.8 %collective-permute-done.5 = f32[1536,256]{1,0:T(8,128)S(1)} collective-permute-done((f32[1536,256]{1,0:T(8,128)S(1)}, f32[1536,256]{1,0:T(8,128)S(1)}, u32[]{:S(2)}, u32[]{:S(2)}) %collective-permute-start.5) | collective-permute-done | bytes 1572896 | tf_op jit(solution)/shard_map/ppermute | solution.py:29
  379.4 28.4 %all-reduce.10.cloned.1.call-done = f32[256,1536]{1,0:T(8,128)} async-done(((f32[256,1536]{1,0:T(8,128)}), f32[256,1536]{1,0:T(8,128)}) %all-reduce.10.cloned.1.call-update) | async-done | bytes 1572880 | tf_op jit(solution)/shard_map/psum | solution.py:205
  407.8 4.6 fusion.2
  412.4 2.4 fusion
  414.8 2.4 fusion.11
  418.3 2.5 collective-permute-done.6
  420.8 1.7 broadcast_select_fusion
  424.1 13.4 %subtract_select_fusion.1 = f32[1536,1536]{1,0:T(8,128)} fusion(f32[1536,1536]{1,0:T(8,128)} %copy-done.4, f32[1536,256]{1,0:T(8,128)S(1)} %broadcast_select_fusion.3, f32[256,1536]{1,0:T(8,128)} %all-reduce.10.cloned.1.call-done, pred[1536]{0:T(1024)(128)(4,1)S(1)} %get-tuple-element.22, pred[1536]{0:T(1024)(128)(4,1)S(1)} %get-tuple-element.21), kind=kOutput, calls=%fused_computation.5 | convolution fusion | flops 7254835200 | bytes 22023168 | tf_op jit(solution)/shard_map/dot_general | solution.py:242
  437.5 2.9 select_dynamic-update-slice_fusion
  440.4 45.3 %all-reduce.12.cloned.1.call-done = f32[256,1536]{1,0:T(8,128)} async-done(((f32[256,1536]{1,0:T(8,128)}), f32[256,1536]{1,0:T(8,128)}) %all-reduce.12.cloned.1.call-update) | async-done | bytes 1572880 | tf_op jit(solution)/shard_map/psum | solution.py:205
  485.8 11.8 %subtract_select_fusion = f32[1536,1536]{1,0:T(8,128)S(1)} fusion(f32[1536,1536]{1,0:T(8,128)} %select_dynamic-update-slice_fusion, f32[256,1536]{1,0:T(8,128)} %all-reduce.12.cloned.1.call-done, pred[1536]{0:T(1024)(128)(4,1)S(1)} %get-tuple-element.20, pred[1536]{0:T(1024)(128)(4,1)S(1)} %get-tuple-element.19, f32[1536,256]{1,0:T(8,128)} %collective-permute-done.7, ...), kind=kOutput, calls=%fused_computation.4 | convolution fusion | flops 7255228416 | bytes 23596032 | tf_op jit(solution)/shard_map/dot_general | solution.py:242
  497.6 3.7 copy.120
  (140 shorter events, 22.5 us)
Async XLA Ops:
  6.5 48.2 %copy-start = (f32[1,6144]{1,0:T(1,128)S(1)}, f32[1,6144]{1,0:T(1,128)}, u32[]{:S(2)}) copy-start(f32[1,6144]{1,0:T(1,128)} %param.11) | copy-start | bytes 73732
  21.8 7.5 %copy-start.10 = (s32[1,2,16]{2,1,0:T(2,128)S(1)}, s32[1,2,16]{2,1,0:T(2,128)}, u32[]{:S(2)}) copy-start(s32[1,2,16]{2,1,0:T(2,128)} %param.8) | copy-start | bytes 388
  21.8 7.6 %copy-start.11 = (s32[1,2,16]{2,1,0:T(2,128)S(1)}, s32[1,2,16]{2,1,0:T(2,128)}, u32[]{:S(2)}) copy-start(s32[1,2,16]{2,1,0:T(2,128)} %param.9) | copy-start | bytes 388
  21.8 7.7 %copy-start.8 = (s32[1,4]{1,0:T(1,128)S(1)}, s32[1,4]{1,0:T(1,128)}, u32[]{:S(2)}) copy-start(s32[1,4]{1,0:T(1,128)} %param.12) | copy-start | bytes 52
  21.8 9.0 %copy-start.12 = (u32[32]{0:T(128)S(1)}, u32[32]{0:T(128)}, u32[]{:S(2)}) copy-start(u32[32]{0:T(128)} %constant.382) | copy-start | bytes 388
  21.8 10.3 %copy-start.9 = (s32[1,2]{1,0:T(1,128)S(1)}, s32[1,2]{1,0:T(1,128)}, u32[]{:S(2)}) copy-start(s32[1,2]{1,0:T(1,128)} %param.10) | copy-start | bytes 28
  21.9 97.9 %all-to-all-start = ((f32[32,2,128,128]{3,2,1,0:T(8,128)}), f32[32,2,128,128]{3,2,1,0:T(8,128)}, u32[]{:S(2)}, u32[]{:S(2)}) async-start(f32[32,2,128,128]{3,2,1,0:T(8,128)} %bitcast.158), calls=%async_computation | async-start | bytes 8388608 | tf_op jit(solution)/shard_map/all_to_all | solution.py:158
  29.3 214.6 %all-reduce.6.cloned.1.call-start = ((), (), s32[]{:S(2)}) async-start(), calls=%async_computation.1 | async-start | bytes 3145728 | tf_op jit(solution)/shard_map/psum | solution.py:205
  157.3 3.7 copy-start.2
  163.8 4.9 collective-permute-start
  168.9 36.7 %collective-permute-start.1 = (f32[1536,256]{1,0:T(8,128)S(1)}, f32[1536,256]{1,0:T(8,128)}, u32[]{:S(2)}, u32[]{:S(2)}) collective-permute-start(f32[1536,256]{1,0:T(8,128)S(1)} %broadcast_select_fusion.6), channel_id=1, source_target_pairs={{0,8},{4,12},{8,0},{12,4},{1,9},{5,13},{9,1},{13,5},{2,10},{6,14},... | collective-permute-start | bytes 4718600 | tf_op jit(solution)/shard_map/ppermute | solution.py:29
  173.2 153.0 %all-reduce.8.cloned.1.call-start = ((), (), s32[]{:S(2)}) async-start(), calls=%async_computation.2 | async-start | bytes 3145728 | tf_op jit(solution)/shard_map/psum | solution.py:205
  243.9 4.7 copy-start.5
  254.9 3.8 collective-permute-start.2
  257.7 150.0 %all-reduce.10.cloned.1.call-start = ((), (), s32[]{:S(2)}) async-start(), calls=%async_computation.3 | async-start | bytes 3145728 | tf_op jit(solution)/shard_map/psum | solution.py:205
  260.3 36.5 %collective-permute-start.3 = (f32[1536,256]{1,0:T(8,128)S(1)}, f32[1536,256]{1,0:T(8,128)S(1)}, u32[]{:S(2)}, u32[]{:S(2)}) collective-permute-start(f32[1536,256]{1,0:T(8,128)S(1)} %broadcast_select_fusion.4), channel_id=1, source_target_pairs={{0,8},{4,12},{8,0},{12,4},{1,9},{5,13},{9,1},{13,5},{2,10},{6,14},... | collective-permute-start | bytes 4718600 | tf_op jit(solution)/shard_map/ppermute | solution.py:29
  274.4 3.7 copy-start.3
  326.2 4.7 copy-start.6
  337.3 3.8 collective-permute-start.4
  339.3 146.4 %all-reduce.12.cloned.1.call-start = ((), (), s32[]{:S(2)}) async-start(), calls=%async_computation.4 | async-start | bytes 3145728 | tf_op jit(solution)/shard_map/psum | solution.py:205
  342.6 36.5 %collective-permute-start.5 = (f32[1536,256]{1,0:T(8,128)S(1)}, f32[1536,256]{1,0:T(8,128)S(1)}, u32[]{:S(2)}, u32[]{:S(2)}) collective-permute-start(f32[1536,256]{1,0:T(8,128)S(1)} %broadcast_select_fusion.2), channel_id=1, source_target_pairs={{0,8},{4,12},{8,0},{12,4},{1,9},{5,13},{9,1},{13,5},{2,10},{6,14},... | collective-permute-start | bytes 4718600 | tf_op jit(solution)/shard_map/ppermute | solution.py:29
  356.4 3.7 copy-start.4
  417.2 1.1 copy-start.7
  417.2 3.6 collective-permute-start.6
  422.5 63.2 %collective-permute-start.7 = (f32[1536,256]{1,0:T(8,128)S(1)}, f32[1536,256]{1,0:T(8,128)}, u32[]{:S(2)}, u32[]{:S(2)}) collective-permute-start(f32[1536,256]{1,0:T(8,128)S(1)} %broadcast_select_fusion), channel_id=1, source_target_pairs={{0,8},{4,12},{8,0},{12,4},{1,9},{5,13},{9,1},{13,5},{2,10},{6,14},... | collective-permute-start | bytes 4718600 | tf_op jit(solution)/shard_map/ppermute | solution.py:29
  501.4 1.5 copy-start.1
Sparse Core Ops, SparseCore 0:
  173.4 70.4 all-reduce.5
  257.9 68.3 all-reduce.7
  339.4 68.3 all-reduce.9
  417.4 68.2 all-reduce.11
